TPU v7x, 128 devices: a whole 4x4x4 slice. The times are simulated.
128 devices in a mesh: row: 8 (over y, core), col: 16 (over x, z).
Axes of the slice: x: 4, y: 4, z: 4, core: 2. Of those that a mesh axis runs over, the one named last changes fastest.
Arguments:
- source_mass: float32 [64, 16, 1024], P('row', None, 'col'), may hold values from 0.3 to 3
- target_mass: float32 [64, 16, 1024], P('col', None, 'row'), may hold values from 0.3 to 3
- tile_list: int32 [8, 16, 8, 2], P('row', 'col'), may hold values from 0 to 63, as said below
- kernel_tiles: bfloat16 [8, 16, 8, 1024, 1024], P('row', 'col'), may hold values from 0.001 to 1
Outputs:
- log_u: float32 [64, 16, 1024], P('row', None, 'col')
- log_v: float32 [64, 16, 1024], P('col', None, 'row')
Inputs may be any that keep to these rules, and one draw needn't show every extreme that they name: `tile_list`: device (i, j) holds 8 distinct tiles whose block rows lie in i * 8 to (i + 1) * 8 - 1 and block columns in j * 4 to (j + 1) * 4 - 1; every block row and every block column has at least one tile; the number of tiles of a block row varies.
All inputs are finite; a program needn't handle non-finite values.
Results may differ from a plain program's by a relative error of at most 0.0003.
Values may be sent and summed in bfloat16 or wider, within the bound.
No kernel may reach another device: no remote copies, remote signals or barrier semaphores. Data moves between devices by JAX's collectives and lax.ppermute only.
A program may use at most 128 MiB of HBM per device.

v0:
```python
import jax
import jax.numpy as jnp
from jax import lax
from jax.sharding import PartitionSpec as P

ITERS = 2


def collect(selector, count, values):
    onehot = (selector[None, :] == jnp.arange(count, dtype=jnp.int32)[:, None]).astype(jnp.float32)
    return jnp.einsum("rt,tcp->rcp", onehot, values, precision=lax.Precision.HIGHEST)


def forward_terms(tiles, target_full, col_local, row_local, count):
    picked = target_full[col_local]
    products = jnp.einsum("tcq,tpq->tcp", picked, tiles, preferred_element_type=jnp.float32)
    return collect(row_local, count, products)


def backward_terms(tiles, source_full, row_local, col_local, count):
    picked = source_full[row_local]
    products = jnp.einsum("tcp,tpq->tcq", picked, tiles, preferred_element_type=jnp.float32)
    return collect(col_local, count, products)


def body(source_mass, target_mass, tile_list, kernel_tiles):
    width = kernel_tiles.shape[-1]
    tiles = kernel_tiles.reshape(-1, width, width)
    listed = tile_list.reshape(-1, 2)
    row_count = source_mass.shape[0]
    col_count = target_mass.shape[0]
    columns = source_mass.shape[1]
    row_local = listed[:, 0] - lax.axis_index("row") * row_count
    col_local = listed[:, 1] - lax.axis_index("col") * col_count
    target_full = jnp.ones((col_count, columns, width), jnp.bfloat16)
    scale_u = source_mass
    scale_v = target_mass
    for step in range(ITERS):
        if step > 0:
            target_full = lax.all_gather(scale_v.astype(jnp.bfloat16), "row", axis=2, tiled=True)
        row_sums = lax.psum_scatter(
            forward_terms(tiles, target_full, col_local, row_local, row_count),
            "col",
            scatter_dimension=2,
            tiled=True,
        )
        scale_u = source_mass / row_sums
        source_full = lax.all_gather(scale_u.astype(jnp.bfloat16), "col", axis=2, tiled=True)
        col_sums = lax.psum_scatter(
            backward_terms(tiles, source_full, row_local, col_local, col_count),
            "row",
            scatter_dimension=2,
            tiled=True,
        )
        scale_v = target_mass / col_sums
    log_u = jnp.log(scale_u)
    log_v = jnp.log(scale_v)
    return (log_u, log_v)


def solution(mesh):
    placed = (
        P("row", None, "col"),
        P("col", None, "row"),
        P("row", "col", None, None),
        P("row", "col", None, None, None),
    )
    return jax.shard_map(
        body,
        mesh=mesh,
        in_specs=placed,
        out_specs=(P("row", None, "col"), P("col", None, "row")),
        check_vma=False,
    )
```

profile of v0, /device:TPU:1, one launch (start us, length us, event | category | flops | bytes accessed | tf_op | source)
XLA Modules:
  0.0 384.7 jit_solution(7333786669863020363)
XLA Ops:
  7.2 0.8 fusion.30
  8.6 10.2 %fusion.6 = f32[8,16,1024]{2,1,0:T(8,128)S(1)} fusion(bf16[8,16,1024]{2,1,0:T(8,128)(2,1)S(1)} %gather_fusion, bf16[1,1,8,1024,1024]{4,3,2,1,0:T(8,128)(2,1)} %param.7), kind=kOutput, calls=%fused_computation.10 | convolution fusion | flops 268435456 | bytes 17563648 | tf_op jit(solution)/shard_map/tcq,tpq->tcp/dot_general | solution.py:16
  18.8 0.7 fusion.14
  19.5 2.7 copy.59
  22.2 3.9 %reshape.60 = f32[1024,128]{1,0:T(8,128)} reshape(f32[1024,8,16]{2,1,0:T(8,128)} %bitcast.44) | data formatting | bytes 1048576
  26.2 75.2 %reduce-scatter.13.cloned.1.call-done = f32[64,128]{1,0:T(8,128)} async-done(((f32[1024,128]{1,0:T(8,128)}), f32[64,128]{1,0:T(8,128)}) %reduce-scatter.13.cloned.1.call-update) | async-done | bytes 32784
  101.5 0.9 reshape.61
  102.7 20.9 %all_gather.9 = bf16[8,16,1024]{1,0,2:T(8,128)(2,1)S(1)} all-gather(bf16[8,16,64]{1,0,2:T(8,128)(2,1)S(1)} %copy.47), channel_id=1, replica_groups=mesh['row'=8,'col'=16] {'col'}, dimensions={2}, use_global_device_ids=true | all-gather | bytes 278528 | tf_op jit(solution)/shard_map/all_gather | solution.py:48
  123.6 1.4 copy.48
  125.6 8.1 %fusion.4 = f32[8,16,1024]{2,1,0:T(8,128)S(1)} fusion(bf16[8,16,1024]{2,1,0:T(8,128)(2,1)S(1)} %gather_fusion.1, bf16[1,1,8,1024,1024]{4,3,2,1,0:T(8,128)(2,1)} %param.7), kind=kOutput, calls=%fused_computation.8 | convolution fusion | flops 268435456 | bytes 17563648 | tf_op jit(solution)/shard_map/tcp,tpq->tcq/dot_general | solution.py:22
  133.7 0.7 fusion.12
  134.3 5.9 %copy.61 = f32[4,16,1024]{0,1,2:T(8,128)} copy(f32[4,16,1024]{2,0,1:T(4,128)S(1)} %fusion.12) | data formatting | bytes 524288
  140.2 7.1 %reshape.62 = f32[1024,64]{1,0:T(8,128)} reshape(f32[1024,16,4]{2,1,0:T(8,128)} %bitcast.41) | data formatting | bytes 524288
  147.5 34.3 %reduce-scatter.15.cloned.1.call-done = f32[128,64]{1,0:T(8,128)} async-done(((f32[1024,64]{1,0:T(8,128)}), f32[128,64]{1,0:T(8,128)}) %reduce-scatter.15.cloned.1.call-update) | async-done | bytes 32784
  181.8 1.4 reshape.63
  183.7 14.4 %all_gather.10 = bf16[4,16,1024]{2,1,0:T(8,128)(2,1)S(1)} all-gather(bf16[4,16,128]{2,1,0:T(8,128)(2,1)S(1)} %divide_convert_fusion.1), channel_id=1, replica_groups=mesh['row'=8,'col'=16] {'row'}, dimensions={2}, use_global_device_ids=true | all-gather | bytes 147456 | tf_op jit(solution)/shard_map/all_gather | solution.py:40
  198.7 10.2 %fusion.2 = f32[8,16,1024]{2,1,0:T(8,128)S(1)} fusion(bf16[8,16,1024]{2,1,0:T(8,128)(2,1)S(1)} %gather_fusion.2, bf16[1,1,8,1024,1024]{4,3,2,1,0:T(8,128)(2,1)} %param.7), kind=kOutput, calls=%fused_computation.6 | convolution fusion | flops 268435456 | bytes 17563648 | tf_op jit(solution)/shard_map/tcq,tpq->tcp/dot_general | solution.py:16
  208.9 0.7 fusion.10
  209.6 5.9 %copy.63 = f32[8,16,1024]{0,1,2:T(8,128)} copy(f32[8,16,1024]{2,0,1:T(8,128)S(1)} %fusion.10) | data formatting | bytes 1048576
  215.5 7.1 %reshape.64 = f32[1024,128]{1,0:T(8,128)} reshape(f32[1024,16,8]{2,1,0:T(8,128)} %bitcast.42) | data formatting | bytes 1048576
  222.6 72.1 %reduce-scatter.17.cloned.1.call-done = f32[64,128]{1,0:T(8,128)} async-done(((f32[1024,128]{1,0:T(8,128)}), f32[64,128]{1,0:T(8,128)}) %reduce-scatter.17.cloned.1.call-update) | async-done | bytes 32784
  294.8 1.0 reshape.65
  296.3 21.1 %all_gather.11 = bf16[8,16,1024]{1,0,2:T(8,128)(2,1)S(1)} all-gather(bf16[8,16,64]{1,0,2:T(8,128)(2,1)S(1)} %copy.53), channel_id=1, replica_groups=mesh['row'=8,'col'=16] {'col'}, dimensions={2}, use_global_device_ids=true | all-gather | bytes 278528 | tf_op jit(solution)/shard_map/all_gather | solution.py:48
  317.3 1.4 copy.54
  319.3 8.1 %fusion = f32[8,16,1024]{2,1,0:T(8,128)S(1)} fusion(bf16[8,16,1024]{2,1,0:T(8,128)(2,1)S(1)} %gather_fusion.3, bf16[1,1,8,1024,1024]{4,3,2,1,0:T(8,128)(2,1)} %param.7), kind=kOutput, calls=%fused_computation.4 | convolution fusion | flops 268435456 | bytes 17563648 | tf_op jit(solution)/shard_map/tcp,tpq->tcq/dot_general | solution.py:22
  327.4 0.7 fusion.8
  328.0 5.9 %copy.65 = f32[4,16,1024]{0,1,2:T(8,128)} copy(f32[4,16,1024]{2,0,1:T(4,128)S(1)} %fusion.8) | data formatting | bytes 524288
  333.9 7.1 %reshape.66 = f32[1024,64]{1,0:T(8,128)} reshape(f32[1024,16,4]{2,1,0:T(8,128)} %bitcast.43) | data formatting | bytes 524288
  341.0 0.6 copy.57
  341.6 34.0 %reduce-scatter.19.cloned.1.call-done = f32[128,64]{1,0:T(8,128)} async-done(((f32[1024,64]{1,0:T(8,128)}), f32[128,64]{1,0:T(8,128)}) %reduce-scatter.19.cloned.1.call-update) | async-done | bytes 32784
  375.6 1.4 reshape.67
  377.5 0.6 copy.58
  (29 shorter events, 4.4 us)
Async XLA Ops:
  7.2 95.3 %copy-start = (f32[8,16,64]{2,1,0:T(8,128)S(1)}, f32[8,16,64]{2,1,0:T(8,128)}, u32[]{:S(2)}) copy-start(f32[8,16,64]{2,1,0:T(8,128)} %param.4) | copy-start | bytes 98308
  7.2 94.3 %reduce-scatter.13.cloned.1.call-start = ((), (), s32[]{:S(2)}) async-start(), calls=%async_computation.4 | async-start | bytes 557056
  26.2 155.7 %reduce-scatter.15.cloned.1.call-start = ((), (), s32[]{:S(2)}) async-start(), calls=%async_computation.5 | async-start | bytes 589824
  125.6 58.1 %copy-start.1 = (f32[4,16,128]{2,1,0:T(8,128)S(1)}, f32[4,16,128]{2,1,0:T(8,128)}, u32[]{:S(2)}) copy-start(f32[4,16,128]{2,1,0:T(8,128)} %param.5) | copy-start | bytes 98308
  147.3 147.5 %reduce-scatter.17.cloned.1.call-start = ((), (), s32[]{:S(2)}) async-start(), calls=%async_computation.6 | async-start | bytes 557056
  222.6 153.0 %reduce-scatter.19.cloned.1.call-start = ((), (), s32[]{:S(2)}) async-start(), calls=%async_computation.7 | async-start | bytes 589824
Sparse Core Ops, SparseCore 0:
  26.3 75.1 reduce-scatter.12
  147.4 34.3 reduce-scatter.14
  222.7 72.0 reduce-scatter.16
  341.1 34.4 reduce-scatter.18
where the time goes:
time: 387 us; the launch traced here: 385 us
  waiting for transfers between devices  216 us (56%)
  local copies, waits for them, and re-layouts  58.1 us (15%)
  blocking collectives  56.4 us (15%)
  matrix products  39.2 us (10%)
  between operations  13.9 us (4%)
    unnamed x8, waiting for transfers between devices  216 us
    unnamed x21, local copies, waits for them, and re-layouts  52.3 us
    all_gather x2, blocking collectives, body(): lax.all_gather(scale_u.astype(jnp.bfloat16), 'col', axis=2, tiled=True)  42 us
    dot_general x2, matrix products, forward_terms(): jnp.einsum('tcq,tpq->tcp', picked, tiles, preferred_element_type=jnp.floa...  20.4 us
    dot_general x2, matrix products, backward_terms(): jnp.einsum('tcp,tpq->tcq', picked, tiles, preferred_element_type=jnp.floa...  16.1 us
    all_gather x1, blocking collectives, body(): lax.all_gather(scale_v.astype(jnp.bfloat16), 'row', axis=2, tiled=True)  14.4 us
  transfers between devices with their start and end apart: 4, of which 4 were waited for; matrix products, arithmetic and copies ran while one was open for 0% of the time, Pallas kernels for 0%

commit v1 on v0

--- a/solution.py
+++ b/solution.py
@@ -23,6 +23,14 @@
     return collect(col_local, count, products)
 
 
+def reduce_scatter(values, axis, parts):
+    lead = values.shape[:-1]
+    width = values.shape[-1] // parts
+    split = values.reshape(lead + (parts, width))
+    moved = lax.all_to_all(split, axis, len(lead), len(lead), tiled=True)
+    return moved.sum(axis=len(lead))
+
+
 def body(source_mass, target_mass, tile_list, kernel_tiles):
     width = kernel_tiles.shape[-1]
     tiles = kernel_tiles.reshape(-1, width, width)
@@ -30,6 +38,8 @@
     row_count = source_mass.shape[0]
     col_count = target_mass.shape[0]
     columns = source_mass.shape[1]
+    n_col = width // source_mass.shape[2]
+    n_row = width // target_mass.shape[2]
     row_local = listed[:, 0] - lax.axis_index("row") * row_count
     col_local = listed[:, 1] - lax.axis_index("col") * col_count
     target_full = jnp.ones((col_count, columns, width), jnp.bfloat16)
@@ -38,19 +48,13 @@
     for step in range(ITERS):
         if step > 0:
             target_full = lax.all_gather(scale_v.astype(jnp.bfloat16), "row", axis=2, tiled=True)
-        row_sums = lax.psum_scatter(
-            forward_terms(tiles, target_full, col_local, row_local, row_count),
-            "col",
-            scatter_dimension=2,
-            tiled=True,
+        row_sums = reduce_scatter(
+            forward_terms(tiles, target_full, col_local, row_local, row_count), "col", n_col
         )
         scale_u = source_mass / row_sums
         source_full = lax.all_gather(scale_u.astype(jnp.bfloat16), "col", axis=2, tiled=True)
-        col_sums = lax.psum_scatter(
-            backward_terms(tiles, source_full, row_local, col_local, col_count),
-            "row",
-            scatter_dimension=2,
-            tiled=True,
+        col_sums = reduce_scatter(
+            backward_terms(tiles, source_full, row_local, col_local, col_count), "row", n_row
         )
         scale_v = target_mass / col_sums
     log_u = jnp.log(scale_u)

time: 387 us -> 178 us (0.46)
  waiting for transfers between devices: 216 us -> 16.2 us
  local copies, waits for them, and re-layouts: 58.1 us -> 12.1 us
  blocking collectives: 56.4 us -> 85.1 us
  starting transfers between devices: 0.35 us -> 19.2 us
  between operations: 13.9 us -> 0.88 us
  other arithmetic: 0.89 us -> 4.91 us
    unnamed x8 -> x0, waiting for transfers between devices: 216 us -> none
    unnamed x21 -> x10, local copies, waits for them, and re-layouts: 52.3 us -> 4.18 us
    all_to_all x0 -> x2, blocking collectives: none -> 31.9 us  [reduce_scatter(): moved = lax.all_to_all(split, axis, len(lead), len(lead), tiled=True)]
    all_to_all x0 -> x2, starting transfers between devices: none -> 19.2 us  [reduce_scatter(): moved = lax.all_to_all(split, axis, len(lead), len(lead), tiled=True)]
    all_to_all x0 -> x2, waiting for transfers between devices: none -> 16.2 us  [reduce_scatter(): moved = lax.all_to_all(split, axis, len(lead), len(lead), tiled=True)]
  transfers between devices with their start and end apart: 4 -> 2, of which waited for: 4 -> 2; matrix products, arithmetic and copies ran while one was open for 0% -> 0% of each run, Pallas kernels for 0% -> 0%
where the time goes in v1:
time: 178 us; the launch traced here: 177 us
  blocking collectives  85.1 us (48%)
  matrix products  39.2 us (22%)
  starting transfers between devices  19.2 us (11%)
  waiting for transfers between devices  16.2 us (9%)
  local copies, waits for them, and re-layouts  12.1 us (7%)
  other arithmetic  4.91 us (3%)
    all_gather x2, blocking collectives, body(): lax.all_gather(scale_u.astype(jnp.bfloat16), 'col', axis=2, tiled=True)  40.8 us
    all_to_all x2, blocking collectives, reduce_scatter(): moved = lax.all_to_all(split, axis, len(lead), len(lead), tiled=True)  31.9 us
    dot_general x2, matrix products, forward_terms(): jnp.einsum('tcq,tpq->tcp', picked, tiles, preferred_element_type=jnp.floa...  20.4 us
    all_to_all x2, starting transfers between devices, reduce_scatter(): moved = lax.all_to_all(split, axis, len(lead), len(lead), tiled=True)  19.2 us
    all_to_all x2, waiting for transfers between devices, reduce_scatter(): moved = lax.all_to_all(split, axis, len(lead), len(lead), tiled=True)  16.2 us
    dot_general x2, matrix products, backward_terms(): jnp.einsum('tcp,tpq->tcq', picked, tiles, preferred_element_type=jnp.floa...  16.1 us
    all_gather x1, blocking collectives, body(): lax.all_gather(scale_v.astype(jnp.bfloat16), 'row', axis=2, tiled=True)  12.4 us
    unnamed x10, local copies, waits for them, and re-layouts  4.18 us
  transfers between devices with their start and end apart: 2, of which 2 were waited for; matrix products, arithmetic and copies ran while one was open for 0% of the time, Pallas kernels for 0%

profile of v1, /device:TPU:1, one launch (start us, length us, event | category | flops | bytes accessed | tf_op | source)
XLA Modules:
  0.0 177.5 jit_solution(920276134529275924)
XLA Ops:
  0.6 0.8 fusion.29
  1.4 0.6 gather_fusion
  2.0 10.2 %fusion.6 = f32[8,16,1024]{2,1,0:T(8,128)S(1)} fusion(bf16[8,16,1024]{2,1,0:T(8,128)(2,1)S(1)} %gather_fusion, bf16[1,1,8,1024,1024]{4,3,2,1,0:T(8,128)(2,1)} %param.7), kind=kOutput, calls=%fused_computation.10 | convolution fusion | flops 268435456 | bytes 17563648 | tf_op jit(solution)/shard_map/tcq,tpq->tcp/dot_general | solution.py:16
  12.2 0.7 fusion.12
  13.5 1.4 reshape.76
  15.0 8.4 %all-to-all-start = ((f32[16,1,8192]{2,1,0:T(1,128)}), f32[16,1,8192]{2,1,0:T(1,128)S(1)}, u32[]{:S(2)}, u32[]{:S(2)}) async-start(f32[16,1,8192]{2,1,0:T(1,128)} %reshape.76), calls=%async_computation | async-start | bytes 1048576 | tf_op jit(solution)/shard_map/all_to_all | solution.py:30
  23.4 10.4 %all-to-all-done = f32[16,1,8192]{2,1,0:T(1,128)S(1)} async-done(((f32[16,1,8192]{2,1,0:T(1,128)}), f32[16,1,8192]{2,1,0:T(1,128)S(1)}, u32[]{:S(2)}, u32[]{:S(2)}) %all-to-all-start) | async-done | bytes 524320 | tf_op jit(solution)/shard_map/all_to_all | solution.py:30
  33.8 0.5 broadcast.46
  34.3 1.9 %reduce = f32[16,8192]{1,0:T(8,128)S(1)} reduce(f32[16,1,8192]{2,1,0:T(1,128)S(1)} %all-to-all-done, f32[]{:T(128)} %broadcast.46), dimensions={1}, to_apply=%all_to_all.12.reduce_sub_computation | reduce | bytes 1048580 | tf_op jit(solution)/shard_map/all_to_all | solution.py:30
  36.9 20.4 %all_gather.9 = bf16[8,16,1024]{1,0,2:T(8,128)(2,1)S(1)} all-gather(bf16[8,16,64]{1,0,2:T(8,128)(2,1)S(1)} %copy.26), channel_id=1, replica_groups=mesh['row'=8,'col'=16] {'col'}, dimensions={2}, use_global_device_ids=true | all-gather | bytes 278528 | tf_op jit(solution)/shard_map/all_gather | solution.py:55
  57.2 1.4 copy.27
  58.6 0.6 gather_fusion.1
  59.2 8.1 %fusion.4 = f32[8,16,1024]{2,1,0:T(8,128)S(1)} fusion(bf16[8,16,1024]{2,1,0:T(8,128)(2,1)S(1)} %gather_fusion.1, bf16[1,1,8,1024,1024]{4,3,2,1,0:T(8,128)(2,1)} %param.7), kind=kOutput, calls=%fused_computation.8 | convolution fusion | flops 268435456 | bytes 17563648 | tf_op jit(solution)/shard_map/tcp,tpq->tcq/dot_general | solution.py:22
  67.3 0.7 convolution_bitcast_fusion.1
  68.0 18.1 %all_to_all.20 = f32[4,16,8,128]{3,0,1,2:T(4,128)S(1)} all-to-all(f32[4,16,8,128]{3,0,1,2:T(4,128)S(1)} %bitcast.56), channel_id=1, replica_groups=mesh['row'=8,'col'=16] {'row'}, dimensions={2} | all-to-all | bytes 524288 | tf_op jit(solution)/shard_map/all_to_all | solution.py:30
  86.2 12.4 %all_gather.10 = bf16[4,16,1024]{2,1,0:T(8,128)(2,1)S(1)} all-gather(bf16[4,16,128]{2,1,0:T(8,128)(2,1)S(1)} %fusion.14), channel_id=1, replica_groups=mesh['row'=8,'col'=16] {'row'}, dimensions={2}, use_global_device_ids=true | all-gather | bytes 147456 | tf_op jit(solution)/shard_map/all_gather | solution.py:50
  98.6 0.6 gather_fusion.2
  99.1 10.2 %fusion.2 = f32[8,16,1024]{2,1,0:T(8,128)S(1)} fusion(bf16[8,16,1024]{2,1,0:T(8,128)(2,1)S(1)} %gather_fusion.2, bf16[1,1,8,1024,1024]{4,3,2,1,0:T(8,128)(2,1)} %param.7), kind=kOutput, calls=%fused_computation.6 | convolution fusion | flops 268435456 | bytes 17563648 | tf_op jit(solution)/shard_map/tcq,tpq->tcp/dot_general | solution.py:16
  109.3 0.7 fusion.9
  110.6 0.7 reshape.78
  111.3 13.8 %all_to_all.21 = f32[16,1,8192]{2,1,0:T(1,128)S(1)} all-to-all(f32[16,1,8192]{2,1,0:T(1,128)S(1)} %reshape.78), channel_id=1, replica_groups=mesh['row'=8,'col'=16] {'col'}, dimensions={0} | all-to-all | bytes 1048576 | tf_op jit(solution)/shard_map/all_to_all | solution.py:30
  125.1 1.9 %reduce.1 = f32[16,8192]{1,0:T(8,128)S(1)} reduce(f32[16,1,8192]{2,1,0:T(1,128)S(1)} %all_to_all.21, f32[]{:T(128)} %broadcast.46), dimensions={1}, to_apply=%all_to_all.14.reduce_sub_computation | reduce | bytes 1048580 | tf_op jit(solution)/shard_map/all_to_all | solution.py:30
  127.6 20.5 %all_gather.11 = bf16[8,16,1024]{1,0,2:T(8,128)(2,1)S(1)} all-gather(bf16[8,16,64]{1,0,2:T(8,128)(2,1)S(1)} %copy.36), channel_id=1, replica_groups=mesh['row'=8,'col'=16] {'col'}, dimensions={2}, use_global_device_ids=true | all-gather | bytes 278528 | tf_op jit(solution)/shard_map/all_gather | solution.py:55
  148.1 1.4 copy.37
  149.5 0.6 gather_fusion.3
  150.1 8.1 %fusion = f32[8,16,1024]{2,1,0:T(8,128)S(1)} fusion(bf16[8,16,1024]{2,1,0:T(8,128)(2,1)S(1)} %gather_fusion.3, bf16[1,1,8,1024,1024]{4,3,2,1,0:T(8,128)(2,1)} %param.7), kind=kOutput, calls=%fused_computation.4 | convolution fusion | flops 268435456 | bytes 17563648 | tf_op jit(solution)/shard_map/tcp,tpq->tcq/dot_general | solution.py:22
  158.1 0.7 convolution_bitcast_fusion
  158.8 0.7 copy.74
  159.6 10.7 %all-to-all-start.3 = ((f32[4,16,8,128]{3,0,1,2:T(4,128)}), f32[4,16,8,128]{3,0,1,2:T(4,128)S(1)}, u32[]{:S(2)}, u32[]{:S(2)}) async-start(f32[4,16,8,128]{3,0,1,2:T(4,128)} %bitcast.50), calls=%async_computation.3 | async-start | bytes 524288 | tf_op jit(solution)/shard_map/all_to_all | solution.py:30
  170.3 0.6 copy.42
  170.9 5.8 %all-to-all-done.3 = f32[4,16,8,128]{3,0,1,2:T(4,128)S(1)} async-done(((f32[4,16,8,128]{3,0,1,2:T(4,128)}), f32[4,16,8,128]{3,0,1,2:T(4,128)S(1)}, u32[]{:S(2)}, u32[]{:S(2)}) %all-to-all-start.3) | async-done | bytes 262176 | tf_op jit(solution)/shard_map/all_to_all | solution.py:30
  176.9 0.6 copy.43
  (24 shorter events, 2.8 us)
Async XLA Ops:
  0.6 36.0 %copy-start = (f32[8,16,64]{2,1,0:T(8,128)S(1)}, f32[8,16,64]{2,1,0:T(8,128)}, u32[]{:S(2)}) copy-start(f32[8,16,64]{2,1,0:T(8,128)} %param.4) | copy-start | bytes 98308
  13.5 72.7 %copy-start.1 = (f32[4,16,128]{2,1,0:T(8,128)S(1)}, f32[4,16,128]{2,1,0:T(8,128)}, u32[]{:S(2)}) copy-start(f32[4,16,128]{2,1,0:T(8,128)} %param.5) | copy-start | bytes 98308
  15.0 18.8 %all-to-all-start = ((f32[16,1,8192]{2,1,0:T(1,128)}), f32[16,1,8192]{2,1,0:T(1,128)S(1)}, u32[]{:S(2)}, u32[]{:S(2)}) async-start(f32[16,1,8192]{2,1,0:T(1,128)} %reshape.76), calls=%async_computation | async-start | bytes 1048576 | tf_op jit(solution)/shard_map/all_to_all | solution.py:30
  159.6 17.2 %all-to-all-start.3 = ((f32[4,16,8,128]{3,0,1,2:T(4,128)}), f32[4,16,8,128]{3,0,1,2:T(4,128)S(1)}, u32[]{:S(2)}, u32[]{:S(2)}) async-start(f32[4,16,8,128]{3,0,1,2:T(4,128)} %bitcast.50), calls=%async_computation.3 | async-start | bytes 524288 | tf_op jit(solution)/shard_map/all_to_all | solution.py:30

commit v2 on v1

--- a/solution.py
+++ b/solution.py
@@ -31,6 +31,13 @@
     return moved.sum(axis=len(lead))
 
 
+def all_gather(values, axis, parts):
+    copies = jnp.broadcast_to(values[None], (parts,) + values.shape)
+    moved = lax.all_to_all(copies, axis, 0, 0, tiled=True)
+    lead = values.shape[:-1]
+    return jnp.moveaxis(moved, 0, -2).reshape(lead + (parts * values.shape[-1],))
+
+
 def body(source_mass, target_mass, tile_list, kernel_tiles):
     width = kernel_tiles.shape[-1]
     tiles = kernel_tiles.reshape(-1, width, width)
@@ -47,12 +54,12 @@
     scale_v = target_mass
     for step in range(ITERS):
         if step > 0:
-            target_full = lax.all_gather(scale_v.astype(jnp.bfloat16), "row", axis=2, tiled=True)
+            target_full = all_gather(scale_v.astype(jnp.bfloat16), "row", n_row)
         row_sums = reduce_scatter(
             forward_terms(tiles, target_full, col_local, row_local, row_count), "col", n_col
         )
         scale_u = source_mass / row_sums
-        source_full = lax.all_gather(scale_u.astype(jnp.bfloat16), "col", axis=2, tiled=True)
+        source_full = all_gather(scale_u.astype(jnp.bfloat16), "col", n_col)
         col_sums = reduce_scatter(
             backward_terms(tiles, source_full, row_local, col_local, col_count), "row", n_row
         )

time: 178 us -> 145 us (0.81)
  starting transfers between devices: 19.2 us -> 6.68 us
  waiting for transfers between devices: 16.2 us -> 5.85 us
  blocking collectives: 85.1 us -> 75.9 us
    all_gather x3 -> x0, blocking collectives: 53.2 us -> none  [the longest x2 40.8 us: body(): lax.all_gather(scale_u.astype(jnp.bfloat16), 'col', axis=2, tiled=True)]
    all_to_all x0 -> x3, blocking collectives: none -> 29.9 us  [all_gather(): moved = lax.all_to_all(copies, axis, 0, 0, tiled=True)]
    all_to_all x2 -> x3, blocking collectives: 31.9 us -> 46 us  [reduce_scatter(): moved = lax.all_to_all(split, axis, len(lead), len(lead), tiled=True)]
    all_to_all x2 -> x1, starting transfers between devices: 19.2 us -> 6.68 us  [reduce_scatter(): moved = lax.all_to_all(split, axis, len(lead), len(lead), tiled=True)]
    all_to_all x2 -> x1, waiting for transfers between devices: 16.2 us -> 5.85 us  [reduce_scatter(): moved = lax.all_to_all(split, axis, len(lead), len(lead), tiled=True)]
    all_gather x2 -> x0, local copies, waits for them, and re-layouts: 2.79 us -> none  [body(): lax.all_gather(scale_u.astype(jnp.bfloat16), 'col', axis=2, tiled=True)]
    unnamed x10 -> x14, local copies, waits for them, and re-layouts: 4.18 us -> 4.87 us
  transfers between devices with their start and end apart: 2 -> 1, of which waited for: 2 -> 1; matrix products, arithmetic and copies ran while one was open for 0% -> 0% of each run, Pallas kernels for 0% -> 0%
where the time goes in v2:
time: 145 us
  blocking collectives  75.9 us (52%)
  matrix products  39.2 us (27%)
  local copies, waits for them, and re-layouts  11.3 us (8%)
  starting transfers between devices  6.68 us (5%)
  waiting for transfers between devices  5.85 us (4%)
  other arithmetic  4.91 us (3%)
    all_to_all x3, blocking collectives, reduce_scatter(): moved = lax.all_to_all(split, axis, len(lead), len(lead), tiled=True)  46 us
    all_to_all x3, blocking collectives, all_gather(): moved = lax.all_to_all(copies, axis, 0, 0, tiled=True)  29.9 us
    dot_general x2, matrix products, forward_terms(): jnp.einsum('tcq,tpq->tcp', picked, tiles, preferred_element_type=jnp.floa...  20.4 us
    dot_general x2, matrix products, backward_terms(): jnp.einsum('tcp,tpq->tcq', picked, tiles, preferred_element_type=jnp.floa...  16.1 us
    all_to_all x1, starting transfers between devices, reduce_scatter(): moved = lax.all_to_all(split, axis, len(lead), len(lead), tiled=True)  6.68 us
    all_to_all x1, waiting for transfers between devices, reduce_scatter(): moved = lax.all_to_all(split, axis, len(lead), len(lead), tiled=True)  5.85 us
    unnamed x14, local copies, waits for them, and re-layouts  4.87 us
    all_to_all x2, other arithmetic, reduce_scatter(): moved = lax.all_to_all(split, axis, len(lead), len(lead), tiled=True)  3.77 us
  transfers between devices with their start and end apart: 1, of which 1 were waited for; matrix products, arithmetic and copies ran while one was open for 0% of the time, Pallas kernels for 0%

profile of v2, /device:TPU:1, one launch (start us, length us, event | category | flops | bytes accessed | tf_op | source)
XLA Modules:
  0.0 144.7 jit_solution(663337290980316791)
XLA Ops:
  0.6 0.8 fusion.29
  1.4 0.6 gather_fusion
  2.0 10.2 %fusion.6 = f32[8,16,1024]{2,1,0:T(8,128)S(1)} fusion(bf16[8,16,1024]{2,1,0:T(8,128)(2,1)S(1)} %gather_fusion, bf16[1,1,8,1024,1024]{4,3,2,1,0:T(8,128)(2,1)} %param.7), kind=kOutput, calls=%fused_computation.10 | convolution fusion | flops 268435456 | bytes 17563648 | tf_op jit(solution)/shard_map/tcq,tpq->tcp/dot_general | solution.py:16
  12.2 0.7 fusion.12
  13.5 0.7 reshape.91
  14.2 18.6 %all_to_all.35 = f32[16,1,8192]{2,1,0:T(1,128)S(1)} all-to-all(f32[16,1,8192]{2,1,0:T(1,128)S(1)} %reshape.91), channel_id=1, replica_groups=mesh['row'=8,'col'=16] {'col'}, dimensions={0} | all-to-all | bytes 1048576 | tf_op jit(solution)/shard_map/all_to_all | solution.py:30
  32.8 0.5 broadcast.49
  33.3 1.9 %reduce = f32[16,8192]{1,0:T(8,128)S(1)} reduce(f32[16,1,8192]{2,1,0:T(1,128)S(1)} %all_to_all.35, f32[]{:T(128)} %broadcast.49), dimensions={1}, to_apply=%all_to_all.21.reduce_sub_computation | reduce | bytes 1048580 | tf_op jit(solution)/shard_map/all_to_all | solution.py:30
  35.2 0.4 reshape.92
  36.2 10.7 %all_to_all.36 = bf16[16,2,4096]{2,1,0:T(2,128)(2,1)S(1)} all-to-all(bf16[16,2,4096]{2,1,0:T(2,128)(2,1)S(1)} %reshape.93), channel_id=1, replica_groups=mesh['row'=8,'col'=16] {'col'}, dimensions={0} | all-to-all | bytes 524288 | tf_op jit(solution)/shard_map/all_to_all | solution.py:36
  47.9 0.6 gather_fusion.1
  48.5 8.1 %fusion.4 = f32[8,16,1024]{2,1,0:T(8,128)S(1)} fusion(bf16[8,16,1024]{2,1,0:T(8,128)(2,1)S(1)} %gather_fusion.1, bf16[1,1,8,1024,1024]{4,3,2,1,0:T(8,128)(2,1)} %param.7), kind=kOutput, calls=%fused_computation.8 | convolution fusion | flops 268435456 | bytes 17563648 | tf_op jit(solution)/shard_map/tcp,tpq->tcq/dot_general | solution.py:22
  56.6 0.7 convolution_bitcast_fusion.1
  57.3 13.9 %all_to_all.37 = f32[4,16,8,128]{3,0,1,2:T(4,128)S(1)} all-to-all(f32[4,16,8,128]{3,0,1,2:T(4,128)S(1)} %bitcast.70), channel_id=1, replica_groups=mesh['row'=8,'col'=16] {'row'}, dimensions={2} | all-to-all | bytes 524288 | tf_op jit(solution)/shard_map/all_to_all | solution.py:30
  71.3 8.7 %all_to_all.38 = bf16[8,4,16,128]{3,2,1,0:T(8,128)(2,1)S(1)} all-to-all(bf16[8,4,16,128]{3,2,1,0:T(8,128)(2,1)S(1)} %broadcast_in_dim.10), channel_id=1, replica_groups=mesh['row'=8,'col'=16] {'row'}, dimensions={0} | all-to-all | bytes 262144 | tf_op jit(solution)/shard_map/all_to_all | solution.py:36
  80.0 0.6 gather_fusion.2
  80.6 10.2 %fusion.2 = f32[8,16,1024]{2,1,0:T(8,128)S(1)} fusion(bf16[8,16,1024]{2,1,0:T(8,128)(2,1)S(1)} %gather_fusion.2, bf16[1,1,8,1024,1024]{4,3,2,1,0:T(8,128)(2,1)} %param.7), kind=kOutput, calls=%fused_computation.6 | convolution fusion | flops 268435456 | bytes 17563648 | tf_op jit(solution)/shard_map/tcq,tpq->tcp/dot_general | solution.py:16
  90.8 0.7 fusion.9
  92.1 0.7 reshape.95
  92.8 13.5 %all_to_all.39 = f32[16,1,8192]{2,1,0:T(1,128)S(1)} all-to-all(f32[16,1,8192]{2,1,0:T(1,128)S(1)} %reshape.95), channel_id=1, replica_groups=mesh['row'=8,'col'=16] {'col'}, dimensions={0} | all-to-all | bytes 1048576 | tf_op jit(solution)/shard_map/all_to_all | solution.py:30
  106.2 1.9 %reduce.1 = f32[16,8192]{1,0:T(8,128)S(1)} reduce(f32[16,1,8192]{2,1,0:T(1,128)S(1)} %all_to_all.39, f32[]{:T(128)} %broadcast.49), dimensions={1}, to_apply=%all_to_all.25.reduce_sub_computation | reduce | bytes 1048580 | tf_op jit(solution)/shard_map/all_to_all | solution.py:30
  108.1 0.4 reshape.96
  108.8 0.4 reshape.97
  109.2 10.6 %all_to_all.40 = bf16[16,2,4096]{2,1,0:T(2,128)(2,1)S(1)} all-to-all(bf16[16,2,4096]{2,1,0:T(2,128)(2,1)S(1)} %reshape.97), channel_id=1, replica_groups=mesh['row'=8,'col'=16] {'col'}, dimensions={0} | all-to-all | bytes 524288 | tf_op jit(solution)/shard_map/all_to_all | solution.py:36
  120.8 0.6 gather_fusion.3
  121.4 8.1 %fusion = f32[8,16,1024]{2,1,0:T(8,128)S(1)} fusion(bf16[8,16,1024]{2,1,0:T(8,128)(2,1)S(1)} %gather_fusion.3, bf16[1,1,8,1024,1024]{4,3,2,1,0:T(8,128)(2,1)} %param.7), kind=kOutput, calls=%fused_computation.4 | convolution fusion | flops 268435456 | bytes 17563648 | tf_op jit(solution)/shard_map/tcp,tpq->tcq/dot_general | solution.py:22
  129.4 0.7 convolution_bitcast_fusion
  130.1 0.7 copy.85
  130.8 6.7 %all-to-all-start.6 = ((f32[4,16,8,128]{3,0,1,2:T(4,128)}), f32[4,16,8,128]{3,0,1,2:T(4,128)S(1)}, u32[]{:S(2)}, u32[]{:S(2)}) async-start(f32[4,16,8,128]{3,0,1,2:T(4,128)} %bitcast.62), calls=%async_computation.6 | async-start | bytes 524288 | tf_op jit(solution)/shard_map/all_to_all | solution.py:30
  137.5 0.6 copy.51
  138.2 5.9 %all-to-all-done.6 = f32[4,16,8,128]{3,0,1,2:T(4,128)S(1)} async-done(((f32[4,16,8,128]{3,0,1,2:T(4,128)}), f32[4,16,8,128]{3,0,1,2:T(4,128)S(1)}, u32[]{:S(2)}, u32[]{:S(2)}) %all-to-all-start.6) | async-done | bytes 262176 | tf_op jit(solution)/shard_map/all_to_all | solution.py:30
  144.1 0.6 copy.52
  (32 shorter events, 4.4 us)
Async XLA Ops:
  0.6 35.1 %copy-start = (f32[8,16,64]{2,1,0:T(8,128)S(1)}, f32[8,16,64]{2,1,0:T(8,128)}, u32[]{:S(2)}) copy-start(f32[8,16,64]{2,1,0:T(8,128)} %param.4) | copy-start | bytes 98308
  13.5 57.8 %copy-start.1 = (f32[4,16,128]{2,1,0:T(8,128)S(1)}, f32[4,16,128]{2,1,0:T(8,128)}, u32[]{:S(2)}) copy-start(f32[4,16,128]{2,1,0:T(8,128)} %param.5) | copy-start | bytes 98308
  130.8 13.2 %all-to-all-start.6 = ((f32[4,16,8,128]{3,0,1,2:T(4,128)}), f32[4,16,8,128]{3,0,1,2:T(4,128)S(1)}, u32[]{:S(2)}, u32[]{:S(2)}) async-start(f32[4,16,8,128]{3,0,1,2:T(4,128)} %bitcast.62), calls=%async_computation.6 | async-start | bytes 524288 | tf_op jit(solution)/shard_map/all_to_all | solution.py:30

commit v3 on v2

--- a/solution.py
+++ b/solution.py
@@ -49,12 +49,21 @@
     n_row = width // target_mass.shape[2]
     row_local = listed[:, 0] - lax.axis_index("row") * row_count
     col_local = listed[:, 1] - lax.axis_index("col") * col_count
-    target_full = jnp.ones((col_count, columns, width), jnp.bfloat16)
-    scale_u = source_mass
-    scale_v = target_mass
-    for step in range(ITERS):
-        if step > 0:
-            target_full = all_gather(scale_v.astype(jnp.bfloat16), "row", n_row)
+    row_part = collect(row_local, row_count, tiles.sum(axis=2, dtype=jnp.float32)[:, None, :])[:, 0, :]
+    payload = jnp.concatenate([source_mass.reshape(-1), row_part.reshape(-1)])
+    copies = jnp.broadcast_to(payload[None], (n_col,) + payload.shape)
+    moved = lax.all_to_all(copies, "col", 0, 0, tiled=True)
+    split = source_mass.size
+    mass_full = jnp.moveaxis(moved[:, :split].reshape((n_col,) + source_mass.shape), 0, 2)
+    mass_full = mass_full.reshape(row_count, columns, width)
+    row_full = moved[:, split:].reshape(n_col, row_count, width).sum(axis=0)
+    source_full = (mass_full / row_full[:, None, :]).astype(jnp.bfloat16)
+    col_sums = reduce_scatter(
+        backward_terms(tiles, source_full, row_local, col_local, col_count), "row", n_row
+    )
+    scale_v = target_mass / col_sums
+    for step in range(1, ITERS):
+        target_full = all_gather(scale_v.astype(jnp.bfloat16), "row", n_row)
         row_sums = reduce_scatter(
             forward_terms(tiles, target_full, col_local, row_local, row_count), "col", n_col
         )

time: 145 us -> 135 us (0.931)
  blocking collectives: 75.9 us -> 37.4 us
  waiting for transfers between devices: 5.85 us -> 26.8 us
  starting transfers between devices: 6.68 us -> 19.5 us
  matrix products: 39.2 us -> 28.5 us
  other arithmetic: 4.91 us -> 9.18 us
    all_to_all x0 -> x2, waiting for transfers between devices: none -> 20.9 us  [the longest x1 15.7 us: body(): moved = lax.all_to_all(copies, 'col', 0, 0, tiled=True)]
    all_to_all x3 -> x1, blocking collectives: 29.9 us -> 10.6 us  [all_gather(): moved = lax.all_to_all(copies, axis, 0, 0, tiled=True)]
    all_to_all x3 -> x2, blocking collectives: 46 us -> 26.8 us  [reduce_scatter(): moved = lax.all_to_all(split, axis, len(lead), len(lead), tiled=True)]
    all_to_all x0 -> x2, starting transfers between devices: none -> 12.9 us  [the longest x1 8.55 us: body(): moved = lax.all_to_all(copies, 'col', 0, 0, tiled=True)]
    dot_general x2 -> x1, matrix products: 20.4 us -> 10.2 us  [forward_terms(): jnp.einsum('tcq,tpq->tcp', picked, tiles, preferred_element_type=jnp.floa...]
    reduce_sum x0 -> x2, other arithmetic: none -> 6.95 us  [the longest x1 6.85 us: body(): tiles.sum(axis=2, dtype=jnp.float32)[:, None, :]]
    all_to_all x2 -> x1, other arithmetic: 3.77 us -> 1.89 us  [reduce_scatter(): moved = lax.all_to_all(split, axis, len(lead), len(lead), tiled=True)]
    broadcast_in_dim x1, local copies, waits for them, and re-layouts: 0.01 us -> 1.8 us  [body(): copies = jnp.broadcast_to(payload[None], (n_col,) + payload.shape)]
  transfers between devices with their start and end apart: 1 -> 3, of which waited for: 1 -> 3; matrix products, arithmetic and copies ran while one was open for 0% -> 0% of each run, Pallas kernels for 0% -> 0%
where the time goes in v3:
time: 135 us; the launch traced here: 134 us
  blocking collectives  37.4 us (28%)
  matrix products  28.5 us (21%)
  waiting for transfers between devices  26.8 us (20%)
  starting transfers between devices  19.5 us (14%)
  local copies, waits for them, and re-layouts  12 us (9%)
  other arithmetic  9.18 us (7%)
    all_to_all x2, blocking collectives, reduce_scatter(): moved = lax.all_to_all(split, axis, len(lead), len(lead), tiled=True)  26.8 us
    dot_general x2, matrix products, backward_terms(): jnp.einsum('tcp,tpq->tcq', picked, tiles, preferred_element_type=jnp.floa...  16.1 us
    all_to_all x1, waiting for transfers between devices, body(): moved = lax.all_to_all(copies, 'col', 0, 0, tiled=True)  15.7 us
    all_to_all x1, blocking collectives, all_gather(): moved = lax.all_to_all(copies, axis, 0, 0, tiled=True)  10.6 us
    dot_general x1, matrix products, forward_terms(): jnp.einsum('tcq,tpq->tcp', picked, tiles, preferred_element_type=jnp.floa...  10.2 us
    all_to_all x1, starting transfers between devices, body(): moved = lax.all_to_all(copies, 'col', 0, 0, tiled=True)  8.55 us
    reduce_sum x1, other arithmetic, body(): tiles.sum(axis=2, dtype=jnp.float32)[:, None, :]  6.85 us
    all_to_all x1, starting transfers between devices, reduce_scatter(): moved = lax.all_to_all(split, axis, len(lead), len(lead), tiled=True)  6.68 us
  transfers between devices with their start and end apart: 3, of which 3 were waited for; matrix products, arithmetic and copies ran while one was open for 0% of the time, Pallas kernels for 0%

profile of v3, /device:TPU:1, one launch (start us, length us, event | category | flops | bytes accessed | tf_op | source)
XLA Modules:
  0.0 134.2 jit_solution(4842673262666309829)
XLA Ops:
  0.7 6.9 %convert_reduce_fusion = f32[8,1024]{1,0:T(8,128)S(1)} fusion(bf16[1,1,8,1024,1024]{4,3,2,1,0:T(8,128)(2,1)} %param.7), kind=kLoop, calls=%fused_computation.3 | loop fusion | flops 16769024 | bytes 16809984 | tf_op jit(solution)/shard_map/reduce_sum | solution.py:52
  7.8 1.8 %broadcast_in_dim.6 = f32[16,1,16384]{2,1,0:T(1,128)} broadcast(f32[16384]{0:T(1024)S(1)} %pad_maximum_fusion), dimensions={2} | broadcast | bytes 1114112 | tf_op jit(solution)/shard_map/broadcast_in_dim | solution.py:54
  9.6 8.5 %all-to-all-start = ((f32[16,1,16384]{2,1,0:T(1,128)}), f32[16,1,16384]{2,1,0:T(1,128)S(1)}, u32[]{:S(2)}, u32[]{:S(2)}) async-start(f32[16,1,16384]{2,1,0:T(1,128)} %broadcast_in_dim.6), calls=%async_computation | async-start | bytes 2097152 | tf_op jit(solution)/shard_map/all_to_all | solution.py:55
  18.2 15.7 %all-to-all-done = f32[16,1,16384]{2,1,0:T(1,128)S(1)} async-done(((f32[16,1,16384]{2,1,0:T(1,128)}), f32[16,1,16384]{2,1,0:T(1,128)S(1)}, u32[]{:S(2)}, u32[]{:S(2)}) %all-to-all-start) | async-done | bytes 1048608 | tf_op jit(solution)/shard_map/all_to_all | solution.py:55
  33.8 0.6 copy.78
  34.5 0.4 reshape.67
  35.0 0.6 copy.29
  36.0 0.6 gather_fusion
  36.5 8.1 %fusion.4 = f32[8,16,1024]{2,1,0:T(8,128)S(1)} fusion(bf16[8,16,1024]{2,1,0:T(8,128)(2,1)S(1)} %gather_fusion, bf16[1,1,8,1024,1024]{4,3,2,1,0:T(8,128)(2,1)} %param.7), kind=kOutput, calls=%fused_computation.8 | convolution fusion | flops 268435456 | bytes 17563648 | tf_op jit(solution)/shard_map/tcp,tpq->tcq/dot_general | solution.py:22
  44.6 0.7 convolution_bitcast_fusion.1
  45.3 13.8 %all_to_all.34 = f32[4,16,8,128]{3,0,1,2:T(4,128)S(1)} all-to-all(f32[4,16,8,128]{3,0,1,2:T(4,128)S(1)} %bitcast.69), channel_id=1, replica_groups=mesh['row'=8,'col'=16] {'row'}, dimensions={2} | all-to-all | bytes 524288 | tf_op jit(solution)/shard_map/all_to_all | solution.py:30
  59.2 0.7 broadcast_in_dim.7
  59.8 4.3 %all-to-all-start.2 = ((bf16[8,4,16,128]{3,2,1,0:T(8,128)(2,1)}), bf16[8,4,16,128]{3,2,1,0:T(8,128)(2,1)S(1)}, u32[]{:S(2)}, u32[]{:S(2)}) async-start(bf16[8,4,16,128]{3,2,1,0:T(8,128)(2,1)} %broadcast_in_dim.7), calls=%async_computation.2 | async-start | bytes 262144 | tf_op jit(solution)/shard_map/all_to_all | solution.py:36
  64.2 5.3 %all-to-all-done.2 = bf16[8,4,16,128]{3,2,1,0:T(8,128)(2,1)S(1)} async-done(((bf16[8,4,16,128]{3,2,1,0:T(8,128)(2,1)}), bf16[8,4,16,128]{3,2,1,0:T(8,128)(2,1)S(1)}, u32[]{:S(2)}, u32[]{:S(2)}) %all-to-all-start.2) | async-done | bytes 131104 | tf_op jit(solution)/shard_map/all_to_all | solution.py:36
  69.4 0.6 gather_fusion.1
  70.0 10.2 %fusion.2 = f32[8,16,1024]{2,1,0:T(8,128)S(1)} fusion(bf16[8,16,1024]{2,1,0:T(8,128)(2,1)S(1)} %gather_fusion.1, bf16[1,1,8,1024,1024]{4,3,2,1,0:T(8,128)(2,1)} %param.7), kind=kOutput, calls=%fused_computation.6 | convolution fusion | flops 268435456 | bytes 17563648 | tf_op jit(solution)/shard_map/tcq,tpq->tcp/dot_general | solution.py:16
  80.2 0.7 fusion.7
  81.5 0.7 reshape.100
  82.2 13.0 %all_to_all.35 = f32[16,1,8192]{2,1,0:T(1,128)S(1)} all-to-all(f32[16,1,8192]{2,1,0:T(1,128)S(1)} %reshape.100), channel_id=1, replica_groups=mesh['row'=8,'col'=16] {'col'}, dimensions={0} | all-to-all | bytes 1048576 | tf_op jit(solution)/shard_map/all_to_all | solution.py:30
  95.2 0.5 broadcast.49
  95.7 1.9 %reduce.1 = f32[16,8192]{1,0:T(8,128)S(1)} reduce(f32[16,1,8192]{2,1,0:T(1,128)S(1)} %all_to_all.35, f32[]{:T(128)} %broadcast.49), dimensions={1}, to_apply=%all_to_all.25.reduce_sub_computation | reduce | bytes 1048580 | tf_op jit(solution)/shard_map/all_to_all | solution.py:30
  97.6 0.4 reshape.101
  98.3 0.4 reshape.102
  98.7 10.6 %all_to_all.36 = bf16[16,2,4096]{2,1,0:T(2,128)(2,1)S(1)} all-to-all(bf16[16,2,4096]{2,1,0:T(2,128)(2,1)S(1)} %reshape.102), channel_id=1, replica_groups=mesh['row'=8,'col'=16] {'col'}, dimensions={0} | all-to-all | bytes 524288 | tf_op jit(solution)/shard_map/all_to_all | solution.py:36
  110.3 0.6 gather_fusion.2
  110.9 8.1 %fusion = f32[8,16,1024]{2,1,0:T(8,128)S(1)} fusion(bf16[8,16,1024]{2,1,0:T(8,128)(2,1)S(1)} %gather_fusion.2, bf16[1,1,8,1024,1024]{4,3,2,1,0:T(8,128)(2,1)} %param.7), kind=kOutput, calls=%fused_computation.4 | convolution fusion | flops 268435456 | bytes 17563648 | tf_op jit(solution)/shard_map/tcp,tpq->tcq/dot_general | solution.py:22
  118.9 0.7 convolution_bitcast_fusion
  119.6 0.7 copy.79
  120.3 6.7 %all-to-all-start.5 = ((f32[4,16,8,128]{3,0,1,2:T(4,128)}), f32[4,16,8,128]{3,0,1,2:T(4,128)S(1)}, u32[]{:S(2)}, u32[]{:S(2)}) async-start(f32[4,16,8,128]{3,0,1,2:T(4,128)} %bitcast.61), calls=%async_computation.5 | async-start | bytes 524288 | tf_op jit(solution)/shard_map/all_to_all | solution.py:30
  127.0 0.6 copy.45
  127.7 5.9 %all-to-all-done.5 = f32[4,16,8,128]{3,0,1,2:T(4,128)S(1)} async-done(((f32[4,16,8,128]{3,0,1,2:T(4,128)}), f32[4,16,8,128]{3,0,1,2:T(4,128)S(1)}, u32[]{:S(2)}, u32[]{:S(2)}) %all-to-all-start.5) | async-done | bytes 262176 | tf_op jit(solution)/shard_map/all_to_all | solution.py:30
  133.6 0.6 copy.46
  (32 shorter events, 2.8 us)
Async XLA Ops:
  0.6 6.9 %copy-start.2 = (s32[1,1,8,2]{2,3,1,0:T(2,128)S(1)}, s32[1,1,8,2]{2,3,1,0:T(2,128)}, u32[]{:S(2)}) copy-start(s32[1,1,8,2]{2,3,1,0:T(2,128)} %param.6) | copy-start | bytes 196
  0.6 7.1 %copy-start = (f32[8,16,64]{2,1,0:T(8,128)S(1)}, f32[8,16,64]{2,1,0:T(8,128)}, u32[]{:S(2)}) copy-start(f32[8,16,64]{2,1,0:T(8,128)} %param.4) | copy-start | bytes 98308
  9.6 49.6 %copy-start.1 = (f32[4,16,128]{2,1,0:T(8,128)S(1)}, f32[4,16,128]{2,1,0:T(8,128)}, u32[]{:S(2)}) copy-start(f32[4,16,128]{2,1,0:T(8,128)} %param.5) | copy-start | bytes 98308
  9.6 24.2 %all-to-all-start = ((f32[16,1,16384]{2,1,0:T(1,128)}), f32[16,1,16384]{2,1,0:T(1,128)S(1)}, u32[]{:S(2)}, u32[]{:S(2)}) async-start(f32[16,1,16384]{2,1,0:T(1,128)} %broadcast_in_dim.6), calls=%async_computation | async-start | bytes 2097152 | tf_op jit(solution)/shard_map/all_to_all | solution.py:55
  59.8 9.6 %all-to-all-start.2 = ((bf16[8,4,16,128]{3,2,1,0:T(8,128)(2,1)}), bf16[8,4,16,128]{3,2,1,0:T(8,128)(2,1)S(1)}, u32[]{:S(2)}, u32[]{:S(2)}) async-start(bf16[8,4,16,128]{3,2,1,0:T(8,128)(2,1)} %broadcast_in_dim.7), calls=%async_computation.2 | async-start | bytes 262144 | tf_op jit(solution)/shard_map/all_to_all | solution.py:36
  120.3 13.2 %all-to-all-start.5 = ((f32[4,16,8,128]{3,0,1,2:T(4,128)}), f32[4,16,8,128]{3,0,1,2:T(4,128)S(1)}, u32[]{:S(2)}, u32[]{:S(2)}) async-start(f32[4,16,8,128]{3,0,1,2:T(4,128)} %bitcast.61), calls=%async_computation.5 | async-start | bytes 524288 | tf_op jit(solution)/shard_map/all_to_all | solution.py:30

commit v4 on v3

--- a/solution.py
+++ b/solution.py
@@ -23,19 +23,25 @@
     return collect(col_local, count, products)
 
 
+LANES = 128
+
+
 def reduce_scatter(values, axis, parts):
     lead = values.shape[:-1]
     width = values.shape[-1] // parts
-    split = values.reshape(lead + (parts, width))
-    moved = lax.all_to_all(split, axis, len(lead), len(lead), tiled=True)
-    return moved.sum(axis=len(lead))
+    split = jnp.moveaxis(values.reshape(lead + (parts, width)), -2, 0)
+    dense = split.reshape(parts, -1, LANES)
+    moved = lax.all_to_all(dense, axis, 0, 0, tiled=True)
+    return moved.sum(axis=0).reshape(lead + (width,))
 
 
 def all_gather(values, axis, parts):
-    copies = jnp.broadcast_to(values[None], (parts,) + values.shape)
+    dense = values.reshape(-1, LANES)
+    copies = jnp.broadcast_to(dense[None], (parts,) + dense.shape)
     moved = lax.all_to_all(copies, axis, 0, 0, tiled=True)
     lead = values.shape[:-1]
-    return jnp.moveaxis(moved, 0, -2).reshape(lead + (parts * values.shape[-1],))
+    moved = jnp.moveaxis(moved.reshape((parts,) + values.shape), 0, -2)
+    return moved.reshape(lead + (parts * values.shape[-1],))
 
 
 def body(source_mass, target_mass, tile_list, kernel_tiles):
@@ -50,9 +56,9 @@
     row_local = listed[:, 0] - lax.axis_index("row") * row_count
     col_local = listed[:, 1] - lax.axis_index("col") * col_count
     row_part = collect(row_local, row_count, tiles.sum(axis=2, dtype=jnp.float32)[:, None, :])[:, 0, :]
-    payload = jnp.concatenate([source_mass.reshape(-1), row_part.reshape(-1)])
+    payload = jnp.concatenate([source_mass.reshape(-1), row_part.reshape(-1)]).reshape(-1, LANES)
     copies = jnp.broadcast_to(payload[None], (n_col,) + payload.shape)
-    moved = lax.all_to_all(copies, "col", 0, 0, tiled=True)
+    moved = lax.all_to_all(copies, "col", 0, 0, tiled=True).reshape(n_col, -1)
     split = source_mass.size
     mass_full = jnp.moveaxis(moved[:, :split].reshape((n_col,) + source_mass.shape), 0, 2)
     mass_full = mass_full.reshape(row_count, columns, width)

time: 135 us -> 128 us (0.948)
  blocking collectives: 37.4 us -> 58.3 us
  waiting for transfers between devices: 26.8 us -> 15.6 us
  starting transfers between devices: 19.5 us -> 8.42 us
  local copies, waits for them, and re-layouts: 12 us -> 7.77 us
    all_to_all x2 -> x3, blocking collectives: 26.8 us -> 39.1 us  [reduce_scatter(): moved = lax.all_to_all(dense, axis, 0, 0, tiled=True)]
    all_to_all x3 -> x1, waiting for transfers between devices: 26.8 us -> 15.6 us  [body(): moved = lax.all_to_all(copies, 'col', 0, 0, tiled=True).reshape(n_col, -1)]
    all_to_all x3 -> x1, starting transfers between devices: 19.5 us -> 8.42 us  [body(): moved = lax.all_to_all(copies, 'col', 0, 0, tiled=True).reshape(n_col, -1)]
    all_to_all x1 -> x2, blocking collectives: 10.6 us -> 19.2 us  [all_gather(): moved = lax.all_to_all(copies, axis, 0, 0, tiled=True)]
    unnamed x14 -> x7, local copies, waits for them, and re-layouts: 3.69 us -> 0.63 us
    all_to_all x1 -> x0, other arithmetic: 1.89 us -> none  [reduce_scatter(): moved = lax.all_to_all(split, axis, len(lead), len(lead), tiled=True)]
  transfers between devices with their start and end apart: 3 -> 1, of which waited for: 3 -> 1; matrix products, arithmetic and copies ran while one was open for 0% -> 0% of each run, Pallas kernels for 0% -> 0%
where the time goes in v4:
time: 128 us
  blocking collectives  58.3 us (46%)
  matrix products  28.5 us (22%)
  waiting for transfers between devices  15.6 us (12%)
  starting transfers between devices  8.42 us (7%)
  other arithmetic  8.41 us (7%)
  local copies, waits for them, and re-layouts  7.77 us (6%)
    all_to_all x3, blocking collectives, reduce_scatter(): moved = lax.all_to_all(dense, axis, 0, 0, tiled=True)  39.1 us
    all_to_all x2, blocking collectives, all_gather(): moved = lax.all_to_all(copies, axis, 0, 0, tiled=True)  19.2 us
    dot_general x2, matrix products, backward_terms(): jnp.einsum('tcp,tpq->tcq', picked, tiles, preferred_element_type=jnp.floa...  16.1 us
    all_to_all x1, waiting for transfers between devices, body(): moved = lax.all_to_all(copies, 'col', 0, 0, tiled=True).reshape(n_col, -1)  15.6 us
    dot_general x1, matrix products, forward_terms(): jnp.einsum('tcq,tpq->tcp', picked, tiles, preferred_element_type=jnp.floa...  10.2 us
    all_to_all x1, starting transfers between devices, body(): moved = lax.all_to_all(copies, 'col', 0, 0, tiled=True).reshape(n_col, -1)  8.42 us
    reduce_sum x1, other arithmetic, body(): tiles.sum(axis=2, dtype=jnp.float32)[:, None, :]  6.85 us
  transfers between devices with their start and end apart: 1, of which 1 were waited for; matrix products, arithmetic and copies ran while one was open for 0% of the time, Pallas kernels for 0%

profile of v4, /device:TPU:1, one launch (start us, length us, event | category | flops | bytes accessed | tf_op | source)
XLA Modules:
  0.0 127.9 jit_solution(9040147327424916811)
XLA Ops:
  0.7 6.9 %convert_reduce_fusion = f32[8,1024]{1,0:T(8,128)S(1)} fusion(bf16[1,1,8,1024,1024]{4,3,2,1,0:T(8,128)(2,1)} %param.7), kind=kLoop, calls=%fused_computation.3 | loop fusion | flops 16769024 | bytes 16809984 | tf_op jit(solution)/shard_map/reduce_sum | solution.py:58
  7.8 1.1 broadcast_in_dim.10
  8.9 8.4 %all-to-all-start = ((f32[16,128,128]{2,1,0:T(8,128)}), f32[16,128,128]{2,1,0:T(8,128)S(1)}, u32[]{:S(2)}, u32[]{:S(2)}) async-start(f32[16,128,128]{2,1,0:T(8,128)} %broadcast_in_dim.10), calls=%async_computation | async-start | bytes 2097152 | tf_op jit(solution)/shard_map/all_to_all | solution.py:61
  17.3 15.6 %all-to-all-done = f32[16,128,128]{2,1,0:T(8,128)S(1)} async-done(((f32[16,128,128]{2,1,0:T(8,128)}), f32[16,128,128]{2,1,0:T(8,128)S(1)}, u32[]{:S(2)}, u32[]{:S(2)}) %all-to-all-start) | async-done | bytes 1048608 | tf_op jit(solution)/shard_map/all_to_all | solution.py:61
  33.0 0.6 copy.36
  33.7 0.4 reshape.91
  34.1 0.6 copy.17
  34.7 0.3 reshape.92
  35.1 0.6 gather_fusion
  35.7 8.1 %fusion.4 = f32[8,16,1024]{2,1,0:T(8,128)S(1)} fusion(bf16[8,16,1024]{2,1,0:T(8,128)(2,1)S(1)} %gather_fusion, bf16[1,1,8,1024,1024]{4,3,2,1,0:T(8,128)(2,1)} %param.7), kind=kOutput, calls=%fused_computation.8 | convolution fusion | flops 268435456 | bytes 17563648 | tf_op jit(solution)/shard_map/tcp,tpq->tcq/dot_general | solution.py:22
  43.8 0.7 fusion.10
  44.5 0.2 copy.19
  44.7 13.8 %all_to_all.30 = f32[8,64,128]{2,1,0:T(8,128)S(1)} all-to-all(f32[8,64,128]{2,1,0:T(8,128)S(1)} %bitcast.69), channel_id=1, replica_groups=mesh['row'=8,'col'=16] {'row'}, dimensions={0} | all-to-all | bytes 524288 | tf_op jit(solution)/shard_map/all_to_all | solution.py:34
  58.6 8.7 %all_to_all.31 = bf16[8,64,128]{2,1,0:T(8,128)(2,1)S(1)} all-to-all(bf16[8,64,128]{2,1,0:T(8,128)(2,1)S(1)} %broadcast_in_dim.12), channel_id=1, replica_groups=mesh['row'=8,'col'=16] {'row'}, dimensions={0} | all-to-all | bytes 262144 | tf_op jit(solution)/shard_map/all_to_all | solution.py:41
  67.4 0.6 gather_fusion.1
  68.0 10.2 %fusion.2 = f32[8,16,1024]{2,1,0:T(8,128)S(1)} fusion(bf16[8,16,1024]{2,1,0:T(8,128)(2,1)S(1)} %gather_fusion.1, bf16[1,1,8,1024,1024]{4,3,2,1,0:T(8,128)(2,1)} %param.7), kind=kOutput, calls=%fused_computation.6 | convolution fusion | flops 268435456 | bytes 17563648 | tf_op jit(solution)/shard_map/tcq,tpq->tcp/dot_general | solution.py:16
  78.2 0.7 fusion.8
  78.8 0.3 reshape.98
  79.1 0.6 copy.37
  79.7 0.2 reshape.99
  80.0 13.0 %all_to_all.32 = f32[16,64,128]{2,1,0:T(8,128)S(1)} all-to-all(f32[16,64,128]{2,1,0:T(8,128)S(1)} %reshape.99), channel_id=1, replica_groups=mesh['row'=8,'col'=16] {'col'}, dimensions={0} | all-to-all | bytes 1048576 | tf_op jit(solution)/shard_map/all_to_all | solution.py:34
  93.1 0.7 divide_convert_fusion.2
  93.9 10.6 %all_to_all.33 = bf16[16,64,128]{2,1,0:T(8,128)(2,1)S(1)} all-to-all(bf16[16,64,128]{2,1,0:T(8,128)(2,1)S(1)} %broadcast_in_dim.14), channel_id=1, replica_groups=mesh['row'=8,'col'=16] {'col'}, dimensions={0} | all-to-all | bytes 524288 | tf_op jit(solution)/shard_map/all_to_all | solution.py:41
  104.5 0.2 reshape.101
  104.7 0.3 copy.23
  105.1 0.3 reshape.102
  105.4 0.6 gather_fusion.2
  106.0 8.1 %fusion = f32[8,16,1024]{2,1,0:T(8,128)S(1)} fusion(bf16[8,16,1024]{2,1,0:T(8,128)(2,1)S(1)} %gather_fusion.2, bf16[1,1,8,1024,1024]{4,3,2,1,0:T(8,128)(2,1)} %param.7), kind=kOutput, calls=%fused_computation.4 | convolution fusion | flops 268435456 | bytes 17563648 | tf_op jit(solution)/shard_map/tcp,tpq->tcq/dot_general | solution.py:22
  114.1 0.7 fusion.6
  114.8 0.2 copy.25
  115.0 12.2 %all_to_all.34 = f32[8,64,128]{2,1,0:T(8,128)S(1)} all-to-all(f32[8,64,128]{2,1,0:T(8,128)S(1)} %bitcast.70), channel_id=1, replica_groups=mesh['row'=8,'col'=16] {'row'}, dimensions={0} | all-to-all | bytes 524288 | tf_op jit(solution)/shard_map/all_to_all | solution.py:34
  127.3 0.6 divide_log_fusion
  (27 shorter events, 1.1 us)
Async XLA Ops:
  0.6 6.9 %copy-start.2 = (s32[1,1,8,2]{2,3,1,0:T(2,128)S(1)}, s32[1,1,8,2]{2,3,1,0:T(2,128)}, u32[]{:S(2)}) copy-start(s32[1,1,8,2]{2,3,1,0:T(2,128)} %param.6) | copy-start | bytes 196
  0.6 7.1 %copy-start = (f32[8,16,64]{2,1,0:T(8,128)S(1)}, f32[8,16,64]{2,1,0:T(8,128)}, u32[]{:S(2)}) copy-start(f32[8,16,64]{2,1,0:T(8,128)} %param.4) | copy-start | bytes 98308
  8.9 24.1 %all-to-all-start = ((f32[16,128,128]{2,1,0:T(8,128)}), f32[16,128,128]{2,1,0:T(8,128)S(1)}, u32[]{:S(2)}, u32[]{:S(2)}) async-start(f32[16,128,128]{2,1,0:T(8,128)} %broadcast_in_dim.10), calls=%async_computation | async-start | bytes 2097152 | tf_op jit(solution)/shard_map/all_to_all | solution.py:61
  17.3 41.2 %copy-start.1 = (f32[4,16,128]{2,1,0:T(8,128)S(1)}, f32[4,16,128]{2,1,0:T(8,128)}, u32[]{:S(2)}) copy-start(f32[4,16,128]{2,1,0:T(8,128)} %param.5) | copy-start | bytes 98308

commit v5 on v4

--- a/solution.py
+++ b/solution.py
@@ -4,6 +4,9 @@
 from jax.sharding import PartitionSpec as P
 
 ITERS = 2
+AR1_TWO_ROUNDS = False
+FWD_TPC = False
+BWD_JS = True
 
 
 def collect(selector, count, values):
@@ -13,11 +16,21 @@
 
 def forward_terms(tiles, target_full, col_local, row_local, count):
     picked = target_full[col_local]
+    if FWD_TPC:
+        products = jnp.einsum("tcq,tpq->tpc", picked, tiles, preferred_element_type=jnp.float32)
+        onehot = (row_local[None, :] == jnp.arange(count, dtype=jnp.int32)[:, None]).astype(jnp.float32)
+        return jnp.einsum("rt,tpc->rcp", onehot, products, precision=lax.Precision.HIGHEST)
     products = jnp.einsum("tcq,tpq->tcp", picked, tiles, preferred_element_type=jnp.float32)
     return collect(row_local, count, products)
 
 
 def backward_terms(tiles, source_full, row_local, col_local, count):
+    if BWD_JS:
+        picked = source_full[:, row_local]
+        parts = picked.shape[0]
+        split_tiles = tiles.reshape(tiles.shape[0], parts, -1, tiles.shape[2])
+        products = jnp.einsum("jtcs,tjsq->tcq", picked, split_tiles, preferred_element_type=jnp.float32)
+        return collect(col_local, count, products)
     picked = source_full[row_local]
     products = jnp.einsum("tcp,tpq->tcq", picked, tiles, preferred_element_type=jnp.float32)
     return collect(col_local, count, products)
@@ -33,6 +46,13 @@
     dense = split.reshape(parts, -1, LANES)
     moved = lax.all_to_all(dense, axis, 0, 0, tiled=True)
     return moved.sum(axis=0).reshape(lead + (width,))
+
+
+def all_gather_parts(values, axis, parts):
+    dense = values.reshape(-1, LANES)
+    copies = jnp.broadcast_to(dense[None], (parts,) + dense.shape)
+    moved = lax.all_to_all(copies, axis, 0, 0, tiled=True)
+    return moved.reshape((parts,) + values.shape)
 
 
 def all_gather(values, axis, parts):
@@ -56,14 +76,26 @@
     row_local = listed[:, 0] - lax.axis_index("row") * row_count
     col_local = listed[:, 1] - lax.axis_index("col") * col_count
     row_part = collect(row_local, row_count, tiles.sum(axis=2, dtype=jnp.float32)[:, None, :])[:, 0, :]
-    payload = jnp.concatenate([source_mass.reshape(-1), row_part.reshape(-1)]).reshape(-1, LANES)
-    copies = jnp.broadcast_to(payload[None], (n_col,) + payload.shape)
-    moved = lax.all_to_all(copies, "col", 0, 0, tiled=True).reshape(n_col, -1)
-    split = source_mass.size
-    mass_full = jnp.moveaxis(moved[:, :split].reshape((n_col,) + source_mass.shape), 0, 2)
-    mass_full = mass_full.reshape(row_count, columns, width)
-    row_full = moved[:, split:].reshape(n_col, row_count, width).sum(axis=0)
-    source_full = (mass_full / row_full[:, None, :]).astype(jnp.bfloat16)
+    if AR1_TWO_ROUNDS:
+        row_own = reduce_scatter(row_part, "col", n_col)
+        scale_1 = source_mass / row_own[:, None, :]
+        if BWD_JS:
+            source_full = all_gather_parts(scale_1.astype(jnp.bfloat16), "col", n_col)
+        else:
+            source_full = all_gather(scale_1.astype(jnp.bfloat16), "col", n_col)
+    else:
+        payload = jnp.concatenate([source_mass.reshape(-1), row_part.reshape(-1)]).reshape(-1, LANES)
+        copies = jnp.broadcast_to(payload[None], (n_col,) + payload.shape)
+        moved = lax.all_to_all(copies, "col", 0, 0, tiled=True).reshape(n_col, -1)
+        split = source_mass.size
+        mass_parts = moved[:, :split].reshape((n_col,) + source_mass.shape)
+        row_full = moved[:, split:].reshape(n_col, row_count, width).sum(axis=0)
+        if BWD_JS:
+            row_parts = jnp.moveaxis(row_full.reshape(row_count, n_col, -1), 1, 0)
+            source_full = (mass_parts / row_parts[:, :, None, :]).astype(jnp.bfloat16)
+        else:
+            mass_full = jnp.moveaxis(mass_parts, 0, 2).reshape(row_count, columns, width)
+            source_full = (mass_full / row_full[:, None, :]).astype(jnp.bfloat16)
     col_sums = reduce_scatter(
         backward_terms(tiles, source_full, row_local, col_local, col_count), "row", n_row
     )
@@ -74,7 +106,10 @@
             forward_terms(tiles, target_full, col_local, row_local, row_count), "col", n_col
         )
         scale_u = source_mass / row_sums
-        source_full = all_gather(scale_u.astype(jnp.bfloat16), "col", n_col)
+        if BWD_JS:
+            source_full = all_gather_parts(scale_u.astype(jnp.bfloat16), "col", n_col)
+        else:
+            source_full = all_gather(scale_u.astype(jnp.bfloat16), "col", n_col)
         col_sums = reduce_scatter(
             backward_terms(tiles, source_full, row_local, col_local, col_count), "row", n_row
         )

time: 128 us -> 125 us (0.977)
  matrix products: 28.5 us -> 26.4 us
  local copies, waits for them, and re-layouts: 7.77 us -> 6.48 us
    all_to_all x0 -> x1, blocking collectives: none -> 10.6 us  [all_gather_parts(): moved = lax.all_to_all(copies, axis, 0, 0, tiled=True)]
    all_to_all x2 -> x1, blocking collectives: 19.2 us -> 8.66 us  [all_gather(): moved = lax.all_to_all(copies, axis, 0, 0, tiled=True)]
    dot_general x2, matrix products: 16.1 us -> 14.1 us  [backward_terms(): jnp.einsum('jtcs,tjsq->tcq', picked, split_tiles, preferred_element_type=...]
where the time goes in v5:
time: 125 us
  blocking collectives  58.3 us (47%)
  matrix products  26.4 us (21%)
  waiting for transfers between devices  15.7 us (13%)
  other arithmetic  8.48 us (7%)
  starting transfers between devices  8.42 us (7%)
  local copies, waits for them, and re-layouts  6.48 us (5%)
    all_to_all x3, blocking collectives, reduce_scatter(): moved = lax.all_to_all(dense, axis, 0, 0, tiled=True)  39 us
    all_to_all x1, waiting for transfers between devices, body(): moved = lax.all_to_all(copies, 'col', 0, 0, tiled=True).reshape(n_col, -1)  15.7 us
    dot_general x2, matrix products, backward_terms(): jnp.einsum('jtcs,tjsq->tcq', picked, split_tiles, preferred_element_type=...  14.1 us
    all_to_all x1, blocking collectives, all_gather_parts(): moved = lax.all_to_all(copies, axis, 0, 0, tiled=True)  10.6 us
    dot_general x1, matrix products, forward_terms(): jnp.einsum('tcq,tpq->tcp', picked, tiles, preferred_element_type=jnp.floa...  10.2 us
    all_to_all x1, blocking collectives, all_gather(): moved = lax.all_to_all(copies, axis, 0, 0, tiled=True)  8.66 us
    all_to_all x1, starting transfers between devices, body(): moved = lax.all_to_all(copies, 'col', 0, 0, tiled=True).reshape(n_col, -1)  8.42 us
    reduce_sum x1, other arithmetic, body(): tiles.sum(axis=2, dtype=jnp.float32)[:, None, :]  6.85 us
  transfers between devices with their start and end apart: 1, of which 1 were waited for; matrix products, arithmetic and copies ran while one was open for 0% of the time, Pallas kernels for 0%

profile of v5, /device:TPU:1, one launch (start us, length us, event | category | flops | bytes accessed | tf_op | source)
XLA Modules:
  0.0 124.6 jit_solution(461471864725705951)
XLA Ops:
  0.7 6.9 %convert_reduce_fusion = f32[8,1024]{1,0:T(8,128)S(1)} fusion(bf16[1,1,8,1024,1024]{4,3,2,1,0:T(8,128)(2,1)} %param.7), kind=kLoop, calls=%fused_computation.3 | loop fusion | flops 16769024 | bytes 16809984 | tf_op jit(solution)/shard_map/reduce_sum | solution.py:78
  7.6 0.1 fusion.11
  7.8 1.1 broadcast_in_dim.10
  8.9 8.4 %all-to-all-start = ((f32[16,128,128]{2,1,0:T(8,128)}), f32[16,128,128]{2,1,0:T(8,128)S(1)}, u32[]{:S(2)}, u32[]{:S(2)}) async-start(f32[16,128,128]{2,1,0:T(8,128)} %broadcast_in_dim.10), calls=%async_computation | async-start | bytes 2097152 | tf_op jit(solution)/shard_map/all_to_all | solution.py:89
  17.3 15.7 %all-to-all-done = f32[16,128,128]{2,1,0:T(8,128)S(1)} async-done(((f32[16,128,128]{2,1,0:T(8,128)}), f32[16,128,128]{2,1,0:T(8,128)S(1)}, u32[]{:S(2)}, u32[]{:S(2)}) %all-to-all-start) | async-done | bytes 1048608 | tf_op jit(solution)/shard_map/all_to_all | solution.py:89
  33.0 0.6 copy.38
  33.7 0.4 reshape.88
  34.2 0.1 divide_convert_fusion
  34.4 0.7 gather_fusion
  35.1 7.0 %convolution_bitcast_fusion.1 = f32[8,16,1024]{2,1,0:T(8,128)S(1)} fusion(bf16[8,16,64,1024]{3,2,1,0:T(8,128)(2,1)} %bitcast.68, bf16[8,16,16,64]{3,2,1,0:T(8,128)(2,1)S(1)} %gather_fusion), kind=kOutput, calls=%fused_computation.7 | convolution fusion | flops 268435456 | bytes 17563648 | tf_op jit(solution)/shard_map/jtcs,tjsq->tcq/dot_general | solution.py:32
  42.1 0.7 fusion.8
  42.8 0.1 reshape.90
  42.9 0.2 copy.20
  43.0 13.8 %all_to_all.30 = f32[8,64,128]{2,1,0:T(8,128)S(1)} all-to-all(f32[8,64,128]{2,1,0:T(8,128)S(1)} %bitcast.73), channel_id=1, replica_groups=mesh['row'=8,'col'=16] {'row'}, dimensions={0} | all-to-all | bytes 524288 | tf_op jit(solution)/shard_map/all_to_all | solution.py:47
  56.9 8.7 %all_to_all.31 = bf16[8,64,128]{2,1,0:T(8,128)(2,1)S(1)} all-to-all(bf16[8,64,128]{2,1,0:T(8,128)(2,1)S(1)} %broadcast_in_dim.12), channel_id=1, replica_groups=mesh['row'=8,'col'=16] {'row'}, dimensions={0} | all-to-all | bytes 262144 | tf_op jit(solution)/shard_map/all_to_all | solution.py:61
  65.7 0.6 gather_fusion.1
  66.3 10.2 %fusion = f32[8,16,1024]{2,1,0:T(8,128)S(1)} fusion(bf16[8,16,1024]{2,1,0:T(8,128)(2,1)S(1)} %gather_fusion.1, bf16[1,1,8,1024,1024]{4,3,2,1,0:T(8,128)(2,1)} %param.7), kind=kOutput, calls=%fused_computation.4 | convolution fusion | flops 268435456 | bytes 17563648 | tf_op jit(solution)/shard_map/tcq,tpq->tcp/dot_general | solution.py:23
  76.5 0.7 fusion.6
  77.2 0.3 reshape.95
  77.5 0.6 copy.39
  78.1 0.2 reshape.96
  78.3 13.0 %all_to_all.32 = f32[16,64,128]{2,1,0:T(8,128)S(1)} all-to-all(f32[16,64,128]{2,1,0:T(8,128)S(1)} %reshape.96), channel_id=1, replica_groups=mesh['row'=8,'col'=16] {'col'}, dimensions={0} | all-to-all | bytes 1048576 | tf_op jit(solution)/shard_map/all_to_all | solution.py:47
  91.4 0.7 divide_convert_fusion.2
  92.2 10.6 %all_to_all.33 = bf16[16,64,128]{2,1,0:T(8,128)(2,1)S(1)} all-to-all(bf16[16,64,128]{2,1,0:T(8,128)(2,1)S(1)} %broadcast_in_dim.14), channel_id=1, replica_groups=mesh['row'=8,'col'=16] {'col'}, dimensions={0} | all-to-all | bytes 524288 | tf_op jit(solution)/shard_map/all_to_all | solution.py:54
  102.8 0.2 reshape.98
  103.1 0.7 gather_fusion.2
  103.7 7.0 %convolution_bitcast_fusion = f32[8,16,1024]{2,1,0:T(8,128)S(1)} fusion(bf16[8,16,64,1024]{3,2,1,0:T(8,128)(2,1)} %bitcast.69, bf16[8,16,16,64]{3,2,1,0:T(8,128)(2,1)S(1)} %gather_fusion.2), kind=kOutput, calls=%fused_computation.6 | convolution fusion | flops 268435456 | bytes 17563648 | tf_op jit(solution)/shard_map/jtcs,tjsq->tcq/dot_general | solution.py:32
  110.8 0.7 fusion.4
  111.4 0.1 reshape.99
  111.6 0.2 copy.25
  111.7 12.2 %all_to_all.34 = f32[8,64,128]{2,1,0:T(8,128)S(1)} all-to-all(f32[8,64,128]{2,1,0:T(8,128)S(1)} %bitcast.74), channel_id=1, replica_groups=mesh['row'=8,'col'=16] {'row'}, dimensions={0} | all-to-all | bytes 524288 | tf_op jit(solution)/shard_map/all_to_all | solution.py:47
  124.0 0.6 divide_log_fusion
  (24 shorter events, 0.8 us)
Async XLA Ops:
  0.6 6.9 %copy-start.2 = (s32[1,1,8,2]{2,3,1,0:T(2,128)S(1)}, s32[1,1,8,2]{2,3,1,0:T(2,128)}, u32[]{:S(2)}) copy-start(s32[1,1,8,2]{2,3,1,0:T(2,128)} %param.6) | copy-start | bytes 196
  0.6 7.1 %copy-start = (f32[8,16,64]{2,1,0:T(8,128)S(1)}, f32[8,16,64]{2,1,0:T(8,128)}, u32[]{:S(2)}) copy-start(f32[8,16,64]{2,1,0:T(8,128)} %param.4) | copy-start | bytes 98308
  7.5 49.3 %copy-start.1 = (f32[4,16,128]{2,1,0:T(8,128)S(1)}, f32[4,16,128]{2,1,0:T(8,128)}, u32[]{:S(2)}) copy-start(f32[4,16,128]{2,1,0:T(8,128)} %param.5) | copy-start | bytes 98308
  8.9 24.1 %all-to-all-start = ((f32[16,128,128]{2,1,0:T(8,128)}), f32[16,128,128]{2,1,0:T(8,128)S(1)}, u32[]{:S(2)}, u32[]{:S(2)}) async-start(f32[16,128,128]{2,1,0:T(8,128)} %broadcast_in_dim.10), calls=%async_computation | async-start | bytes 2097152 | tf_op jit(solution)/shard_map/all_to_all | solution.py:89

commit v6 on v5

--- a/solution.py
+++ b/solution.py
@@ -7,6 +7,9 @@
 AR1_TWO_ROUNDS = False
 FWD_TPC = False
 BWD_JS = True
+MASS_APART = False
+ONEHOT_PICK = True
+FWD_T = False
 
 
 def collect(selector, count, values):
@@ -14,8 +17,25 @@
     return jnp.einsum("rt,tcp->rcp", onehot, values, precision=lax.Precision.HIGHEST)
 
 
+def pick(values, selector, axis):
+    if not ONEHOT_PICK:
+        return values[selector] if axis == 0 else values[:, selector]
+    onehot = (selector[:, None] == jnp.arange(values.shape[axis], dtype=jnp.int32)[None, :]).astype(values.dtype)
+    moved = jnp.moveaxis(values, axis, 0)
+    chosen = jnp.tensordot(onehot, moved, axes=1, preferred_element_type=jnp.float32).astype(values.dtype)
+    return jnp.moveaxis(chosen, 0, axis)
+
+
+def forward_terms_t(tiles_t, target_parts, col_local, row_local, count):
+    picked = pick(target_parts, col_local, 1)
+    parts = picked.shape[0]
+    split_tiles = tiles_t.reshape(tiles_t.shape[0], parts, -1, tiles_t.shape[2])
+    products = jnp.einsum("itcs,tisp->tcp", picked, split_tiles, preferred_element_type=jnp.float32)
+    return collect(row_local, count, products)
+
+
 def forward_terms(tiles, target_full, col_local, row_local, count):
-    picked = target_full[col_local]
+    picked = pick(target_full, col_local, 0)
     if FWD_TPC:
         products = jnp.einsum("tcq,tpq->tpc", picked, tiles, preferred_element_type=jnp.float32)
         onehot = (row_local[None, :] == jnp.arange(count, dtype=jnp.int32)[:, None]).astype(jnp.float32)
@@ -26,7 +46,7 @@
 
 def backward_terms(tiles, source_full, row_local, col_local, count):
     if BWD_JS:
-        picked = source_full[:, row_local]
+        picked = pick(source_full, row_local, 1)
         parts = picked.shape[0]
         split_tiles = tiles.reshape(tiles.shape[0], parts, -1, tiles.shape[2])
         products = jnp.einsum("jtcs,tjsq->tcq", picked, split_tiles, preferred_element_type=jnp.float32)
@@ -84,12 +104,16 @@
         else:
             source_full = all_gather(scale_1.astype(jnp.bfloat16), "col", n_col)
     else:
-        payload = jnp.concatenate([source_mass.reshape(-1), row_part.reshape(-1)]).reshape(-1, LANES)
-        copies = jnp.broadcast_to(payload[None], (n_col,) + payload.shape)
-        moved = lax.all_to_all(copies, "col", 0, 0, tiled=True).reshape(n_col, -1)
-        split = source_mass.size
-        mass_parts = moved[:, :split].reshape((n_col,) + source_mass.shape)
-        row_full = moved[:, split:].reshape(n_col, row_count, width).sum(axis=0)
+        if MASS_APART:
+            mass_parts = all_gather_parts(source_mass, "col", n_col)
+            row_full = all_gather_parts(row_part, "col", n_col).sum(axis=0)
+        else:
+            payload = jnp.concatenate([source_mass.reshape(-1), row_part.reshape(-1)]).reshape(-1, LANES)
+            copies = jnp.broadcast_to(payload[None], (n_col,) + payload.shape)
+            moved = lax.all_to_all(copies, "col", 0, 0, tiled=True).reshape(n_col, -1)
+            split = source_mass.size
+            mass_parts = moved[:, :split].reshape((n_col,) + source_mass.shape)
+            row_full = moved[:, split:].reshape(n_col, row_count, width).sum(axis=0)
         if BWD_JS:
             row_parts = jnp.moveaxis(row_full.reshape(row_count, n_col, -1), 1, 0)
             source_full = (mass_parts / row_parts[:, :, None, :]).astype(jnp.bfloat16)
@@ -100,11 +124,16 @@
         backward_terms(tiles, source_full, row_local, col_local, col_count), "row", n_row
     )
     scale_v = target_mass / col_sums
+    if FWD_T:
+        tiles_t = lax.optimization_barrier(jnp.swapaxes(tiles, 1, 2))
     for step in range(1, ITERS):
-        target_full = all_gather(scale_v.astype(jnp.bfloat16), "row", n_row)
-        row_sums = reduce_scatter(
-            forward_terms(tiles, target_full, col_local, row_local, row_count), "col", n_col
-        )
+        if FWD_T:
+            target_parts = all_gather_parts(scale_v.astype(jnp.bfloat16), "row", n_row)
+            terms = forward_terms_t(tiles_t, target_parts, col_local, row_local, row_count)
+        else:
+            target_full = all_gather(scale_v.astype(jnp.bfloat16), "row", n_row)
+            terms = forward_terms(tiles, target_full, col_local, row_local, row_count)
+        row_sums = reduce_scatter(terms, "col", n_col)
         scale_u = source_mass / row_sums
         if BWD_JS:
             source_full = all_gather_parts(scale_u.astype(jnp.bfloat16), "col", n_col)

time: 125 us -> 123 us (0.984)
  blocking collectives: 58.3 us -> 81.9 us
  waiting for transfers between devices: 15.7 us -> 0 us
  starting transfers between devices: 8.42 us -> 0 us
  local copies, waits for them, and re-layouts: 6.48 us -> 4.4 us
    all_to_all x0 -> x1, blocking collectives: none -> 24.2 us  [body(): moved = lax.all_to_all(copies, 'col', 0, 0, tiled=True).reshape(n_col, -1)]
    all_to_all x1 -> x0, waiting for transfers between devices: 15.7 us -> none  [body(): moved = lax.all_to_all(copies, 'col', 0, 0, tiled=True).reshape(n_col, -1)]
    all_to_all x1 -> x0, starting transfers between devices: 8.42 us -> none  [body(): moved = lax.all_to_all(copies, 'col', 0, 0, tiled=True).reshape(n_col, -1)]
    gather x3 -> x0, local copies, waits for them, and re-layouts: 1.92 us -> none  [the longest x2 1.36 us: backward_terms(): picked = source_full[:, row_local]]
  transfers between devices with their start and end apart: 1 -> 0, of which waited for: 1 -> 0; matrix products, arithmetic and copies ran while one was open for 0% -> 0% of each run, Pallas kernels for 0% -> 0%
where the time goes in v6:
time: 123 us
  blocking collectives  81.9 us (67%)
  matrix products  27.4 us (22%)
  other arithmetic  8.44 us (7%)
  local copies, waits for them, and re-layouts  4.4 us (4%)
    all_to_all x3, blocking collectives, reduce_scatter(): moved = lax.all_to_all(dense, axis, 0, 0, tiled=True)  38.5 us
    all_to_all x1, blocking collectives, body(): moved = lax.all_to_all(copies, 'col', 0, 0, tiled=True).reshape(n_col, -1)  24.2 us
    dot_general x2, matrix products, backward_terms(): jnp.einsum('jtcs,tjsq->tcq', picked, split_tiles, preferred_element_type=...  14.1 us
    all_to_all x1, blocking collectives, all_gather_parts(): moved = lax.all_to_all(copies, axis, 0, 0, tiled=True)  10.6 us
    dot_general x1, matrix products, forward_terms(): jnp.einsum('tcq,tpq->tcp', picked, tiles, preferred_element_type=jnp.floa...  10.2 us
    all_to_all x1, blocking collectives, all_gather(): moved = lax.all_to_all(copies, axis, 0, 0, tiled=True)  8.66 us
    reduce_sum x1, other arithmetic, body(): tiles.sum(axis=2, dtype=jnp.float32)[:, None, :]  6.82 us

profile of v6, /device:TPU:1, one launch (start us, length us, event | category | flops | bytes accessed | tf_op | source)
XLA Modules:
  0.0 123.0 jit_solution(6574554246520989333)
XLA Ops:
  0.6 0.9 concatenate.8
  1.6 6.8 %convert_reduce_fusion = f32[8,1024]{1,0:T(8,128)S(1)} fusion(bf16[1,1,8,1024,1024]{4,3,2,1,0:T(8,128)(2,1)} %param.7), kind=kLoop, calls=%fused_computation | loop fusion | flops 16769024 | bytes 16809984 | tf_op jit(solution)/shard_map/reduce_sum | solution.py:98
  8.4 0.1 fusion.19
  8.7 24.2 %all_to_all.30 = f32[16,128,128]{2,1,0:T(8,128)S(1)} all-to-all(f32[16,128,128]{2,1,0:T(8,128)S(1)} %broadcast_in_dim.10), channel_id=1, replica_groups=mesh['row'=8,'col'=16] {'col'}, dimensions={0} | all-to-all | bytes 2097152 | tf_op jit(solution)/shard_map/all_to_all | solution.py:113
  32.9 0.6 copy.63
  33.5 0.1 slice_reduce_fusion
  33.7 0.4 reshape.88
  34.1 0.1 fusion.15
  34.2 0.4 fusion.2
  34.6 7.0 %convolution_bitcast_fusion.1 = f32[8,16,1024]{2,1,0:T(8,128)S(1)} fusion(bf16[8,16,64,1024]{3,2,1,0:T(8,128)(2,1)} %bitcast.75, bf16[16,8,16,64]{3,1,2,0:T(8,128)(2,1)S(1)} %fusion.2), kind=kOutput, calls=%fused_computation.6 | convolution fusion | flops 268435456 | bytes 17563648 | tf_op jit(solution)/shard_map/jtcs,tjsq->tcq/dot_general | solution.py:52
  41.6 0.7 fusion.11
  42.3 0.1 reshape.90
  42.4 0.2 copy.26
  42.6 12.6 %all_to_all.31 = f32[8,64,128]{2,1,0:T(8,128)S(1)} all-to-all(f32[8,64,128]{2,1,0:T(8,128)S(1)} %bitcast.80), channel_id=1, replica_groups=mesh['row'=8,'col'=16] {'row'}, dimensions={0} | all-to-all | bytes 524288 | tf_op jit(solution)/shard_map/all_to_all | solution.py:67
  55.3 8.7 %all_to_all.32 = bf16[8,64,128]{2,1,0:T(8,128)(2,1)S(1)} all-to-all(bf16[8,64,128]{2,1,0:T(8,128)(2,1)S(1)} %broadcast_in_dim.12), channel_id=1, replica_groups=mesh['row'=8,'col'=16] {'row'}, dimensions={0} | all-to-all | bytes 262144 | tf_op jit(solution)/shard_map/all_to_all | solution.py:81
  64.1 0.3 convolution_convert_fusion.2
  64.4 10.2 %fusion = f32[8,16,1024]{2,1,0:T(8,128)S(1)} fusion(bf16[1,1,8,1024,1024]{4,3,2,1,0:T(8,128)(2,1)} %param.7, bf16[8,16,1024]{2,0,1:T(8,128)(2,1)S(1)} %convolution_convert_fusion.2), kind=kOutput, calls=%fused_computation.1 | convolution fusion | flops 268435456 | bytes 17563648 | tf_op jit(solution)/shard_map/tcq,tpq->tcp/dot_general | solution.py:43
  74.6 0.7 fusion.9
  75.3 0.3 reshape.95
  75.5 0.6 copy.64
  76.2 0.2 reshape.96
  76.4 13.6 %all_to_all.33 = f32[16,64,128]{2,1,0:T(8,128)S(1)} all-to-all(f32[16,64,128]{2,1,0:T(8,128)S(1)} %reshape.96), channel_id=1, replica_groups=mesh['row'=8,'col'=16] {'col'}, dimensions={0} | all-to-all | bytes 1048576 | tf_op jit(solution)/shard_map/all_to_all | solution.py:67
  90.1 0.7 divide_convert_fusion.2
  90.9 10.6 %all_to_all.34 = bf16[16,64,128]{2,1,0:T(8,128)(2,1)S(1)} all-to-all(bf16[16,64,128]{2,1,0:T(8,128)(2,1)S(1)} %broadcast_in_dim.14), channel_id=1, replica_groups=mesh['row'=8,'col'=16] {'col'}, dimensions={0} | all-to-all | bytes 524288 | tf_op jit(solution)/shard_map/all_to_all | solution.py:74
  101.5 0.2 reshape.98
  101.7 0.4 fusion.3
  102.1 7.0 %convolution_bitcast_fusion = f32[8,16,1024]{2,1,0:T(8,128)S(1)} fusion(bf16[8,16,64,1024]{3,2,1,0:T(8,128)(2,1)} %bitcast.76, bf16[16,8,16,64]{3,1,2,0:T(8,128)(2,1)S(1)} %fusion.3), kind=kOutput, calls=%fused_computation.5 | convolution fusion | flops 268435456 | bytes 17563648 | tf_op jit(solution)/shard_map/jtcs,tjsq->tcq/dot_general | solution.py:52
  109.1 0.7 fusion.5
  109.8 0.1 reshape.99
  109.9 0.2 copy.35
  110.1 12.2 %all_to_all.35 = f32[8,64,128]{2,1,0:T(8,128)S(1)} all-to-all(f32[8,64,128]{2,1,0:T(8,128)S(1)} %bitcast.81), channel_id=1, replica_groups=mesh['row'=8,'col'=16] {'row'}, dimensions={0} | all-to-all | bytes 524288 | tf_op jit(solution)/shard_map/all_to_all | solution.py:67
  122.3 0.6 divide_log_fusion
  (22 shorter events, 0.7 us)
Async XLA Ops:
  0.6 7.8 %copy-start.2 = (s32[1,1,8,2]{2,3,1,0:T(2,128)S(1)}, s32[1,1,8,2]{2,3,1,0:T(2,128)}, u32[]{:S(2)}) copy-start(s32[1,1,8,2]{2,3,1,0:T(2,128)} %param.6) | copy-start | bytes 196
  8.4 46.8 %copy-start.1 = (f32[4,16,128]{2,1,0:T(8,128)S(1)}, f32[4,16,128]{2,1,0:T(8,128)}, u32[]{:S(2)}) copy-start(f32[4,16,128]{2,1,0:T(8,128)} %param.5) | copy-start | bytes 98308
  41.6 48.5 %copy-start = (f32[8,16,64]{2,1,0:T(8,128)S(1)}, f32[8,16,64]{2,1,0:T(8,128)}, u32[]{:S(2)}) copy-start(f32[8,16,64]{2,1,0:T(8,128)} %param.4) | copy-start | bytes 98308

commit v7 on v4

--- a/solution.py
+++ b/solution.py
@@ -4,6 +4,7 @@
 from jax.sharding import PartitionSpec as P
 
 ITERS = 2
+LANES = 128
 
 
 def collect(selector, count, values):
@@ -11,19 +12,25 @@
     return jnp.einsum("rt,tcp->rcp", onehot, values, precision=lax.Precision.HIGHEST)
 
 
+def pick(values, selector, axis):
+    onehot = (selector[:, None] == jnp.arange(values.shape[axis], dtype=jnp.int32)[None, :]).astype(values.dtype)
+    moved = jnp.moveaxis(values, axis, 0)
+    chosen = jnp.tensordot(onehot, moved, axes=1, preferred_element_type=jnp.float32).astype(values.dtype)
+    return jnp.moveaxis(chosen, 0, axis)
+
+
 def forward_terms(tiles, target_full, col_local, row_local, count):
-    picked = target_full[col_local]
+    picked = pick(target_full, col_local, 0)
     products = jnp.einsum("tcq,tpq->tcp", picked, tiles, preferred_element_type=jnp.float32)
     return collect(row_local, count, products)
 
 
-def backward_terms(tiles, source_full, row_local, col_local, count):
-    picked = source_full[row_local]
-    products = jnp.einsum("tcp,tpq->tcq", picked, tiles, preferred_element_type=jnp.float32)
+def backward_terms(tiles, source_parts, row_local, col_local, count):
+    picked = pick(source_parts, row_local, 1)
+    parts = picked.shape[0]
+    split_tiles = tiles.reshape(tiles.shape[0], parts, -1, tiles.shape[2])
+    products = jnp.einsum("jtcs,tjsq->tcq", picked, split_tiles, preferred_element_type=jnp.float32)
     return collect(col_local, count, products)
-
-
-LANES = 128
 
 
 def reduce_scatter(values, axis, parts):
@@ -35,13 +42,16 @@
     return moved.sum(axis=0).reshape(lead + (width,))
 
 
-def all_gather(values, axis, parts):
+def all_gather_parts(values, axis, parts):
     dense = values.reshape(-1, LANES)
     copies = jnp.broadcast_to(dense[None], (parts,) + dense.shape)
     moved = lax.all_to_all(copies, axis, 0, 0, tiled=True)
-    lead = values.shape[:-1]
-    moved = jnp.moveaxis(moved.reshape((parts,) + values.shape), 0, -2)
-    return moved.reshape(lead + (parts * values.shape[-1],))
+    return moved.reshape((parts,) + values.shape)
+
+
+def all_gather(values, axis, parts):
+    moved = jnp.moveaxis(all_gather_parts(values, axis, parts), 0, -2)
+    return moved.reshape(values.shape[:-1] + (parts * values.shape[-1],))
 
 
 def body(source_mass, target_mass, tile_list, kernel_tiles):
@@ -50,7 +60,6 @@
     listed = tile_list.reshape(-1, 2)
     row_count = source_mass.shape[0]
     col_count = target_mass.shape[0]
-    columns = source_mass.shape[1]
     n_col = width // source_mass.shape[2]
     n_row = width // target_mass.shape[2]
     row_local = listed[:, 0] - lax.axis_index("row") * row_count
@@ -60,12 +69,12 @@
     copies = jnp.broadcast_to(payload[None], (n_col,) + payload.shape)
     moved = lax.all_to_all(copies, "col", 0, 0, tiled=True).reshape(n_col, -1)
     split = source_mass.size
-    mass_full = jnp.moveaxis(moved[:, :split].reshape((n_col,) + source_mass.shape), 0, 2)
-    mass_full = mass_full.reshape(row_count, columns, width)
+    mass_parts = moved[:, :split].reshape((n_col,) + source_mass.shape)
     row_full = moved[:, split:].reshape(n_col, row_count, width).sum(axis=0)
-    source_full = (mass_full / row_full[:, None, :]).astype(jnp.bfloat16)
+    row_parts = jnp.moveaxis(row_full.reshape(row_count, n_col, -1), 1, 0)
+    source_parts = (mass_parts / row_parts[:, :, None, :]).astype(jnp.bfloat16)
     col_sums = reduce_scatter(
-        backward_terms(tiles, source_full, row_local, col_local, col_count), "row", n_row
+        backward_terms(tiles, source_parts, row_local, col_local, col_count), "row", n_row
     )
     scale_v = target_mass / col_sums
     for step in range(1, ITERS):
@@ -74,9 +83,9 @@
             forward_terms(tiles, target_full, col_local, row_local, row_count), "col", n_col
         )
         scale_u = source_mass / row_sums
-        source_full = all_gather(scale_u.astype(jnp.bfloat16), "col", n_col)
+        source_parts = all_gather_parts(scale_u.astype(jnp.bfloat16), "col", n_col)
         col_sums = reduce_scatter(
-            backward_terms(tiles, source_full, row_local, col_local, col_count), "row", n_row
+            backward_terms(tiles, source_parts, row_local, col_local, col_count), "row", n_row
         )
         scale_v = target_mass / col_sums
     log_u = jnp.log(scale_u)

time: 128 us -> 123 us (0.961)
  blocking collectives: 58.3 us -> 81.9 us
  waiting for transfers between devices: 15.6 us -> 0 us
  starting transfers between devices: 8.42 us -> 0 us
  local copies, waits for them, and re-layouts: 7.77 us -> 4.4 us
    all_to_all x2 -> x3, blocking collectives: 19.2 us -> 43.4 us  [the longest x1 24.2 us: body(): moved = lax.all_to_all(copies, 'col', 0, 0, tiled=True).reshape(n_col, -1)]
    all_to_all x1 -> x0, waiting for transfers between devices: 15.6 us -> none  [body(): moved = lax.all_to_all(copies, 'col', 0, 0, tiled=True).reshape(n_col, -1)]
    all_to_all x1 -> x0, starting transfers between devices: 8.42 us -> none  [body(): moved = lax.all_to_all(copies, 'col', 0, 0, tiled=True).reshape(n_col, -1)]
    gather x3 -> x0, local copies, waits for them, and re-layouts: 1.69 us -> none  [the longest x2 1.13 us: backward_terms(): picked = source_full[row_local]]
    dot_general x2 -> x5, matrix products: 16.1 us -> 15.1 us  [the longest x2 14.1 us: backward_terms(): jnp.einsum('jtcs,tjsq->tcq', picked, split_tiles, preferred_element_type=...]
  transfers between devices with their start and end apart: 1 -> 0, of which waited for: 1 -> 0; matrix products, arithmetic and copies ran while one was open for 0% -> 0% of each run, Pallas kernels for 0% -> 0%
where the time goes in v7:
time: 123 us
  blocking collectives  81.9 us (67%)
  matrix products  27.4 us (22%)
  other arithmetic  8.44 us (7%)
  local copies, waits for them, and re-layouts  4.4 us (4%)
    all_to_all x3, blocking collectives, reduce_scatter(): moved = lax.all_to_all(dense, axis, 0, 0, tiled=True)  38.5 us
    all_to_all x1, blocking collectives, body(): moved = lax.all_to_all(copies, 'col', 0, 0, tiled=True).reshape(n_col, -1)  24.2 us
    all_to_all x2, blocking collectives, all_gather_parts(): moved = lax.all_to_all(copies, axis, 0, 0, tiled=True)  19.2 us
    dot_general x2, matrix products, backward_terms(): jnp.einsum('jtcs,tjsq->tcq', picked, split_tiles, preferred_element_type=...  14.1 us
    dot_general x1, matrix products, forward_terms(): jnp.einsum('tcq,tpq->tcp', picked, tiles, preferred_element_type=jnp.floa...  10.2 us
    reduce_sum x1, other arithmetic, body(): tiles.sum(axis=2, dtype=jnp.float32)[:, None, :]  6.82 us

profile of v7, /device:TPU:1, one launch (start us, length us, event | category | flops | bytes accessed | tf_op | source)
XLA Modules:
  0.0 123.0 jit_solution(6574554246520989333)
XLA Ops:
  0.6 0.9 concatenate.8
  1.6 6.8 %convert_reduce_fusion = f32[8,1024]{1,0:T(8,128)S(1)} fusion(bf16[1,1,8,1024,1024]{4,3,2,1,0:T(8,128)(2,1)} %param.7), kind=kLoop, calls=%fused_computation | loop fusion | flops 16769024 | bytes 16809984 | tf_op jit(solution)/shard_map/reduce_sum | solution.py:67
  8.4 0.1 fusion.19
  8.7 24.2 %all_to_all.30 = f32[16,128,128]{2,1,0:T(8,128)S(1)} all-to-all(f32[16,128,128]{2,1,0:T(8,128)S(1)} %broadcast_in_dim.10), channel_id=1, replica_groups=mesh['row'=8,'col'=16] {'col'}, dimensions={0} | all-to-all | bytes 2097152 | tf_op jit(solution)/shard_map/all_to_all | solution.py:70
  32.9 0.6 copy.63
  33.5 0.1 slice_reduce_fusion
  33.7 0.4 reshape.88
  34.1 0.1 fusion.15
  34.2 0.4 fusion.2
  34.6 7.0 %convolution_bitcast_fusion.1 = f32[8,16,1024]{2,1,0:T(8,128)S(1)} fusion(bf16[8,16,64,1024]{3,2,1,0:T(8,128)(2,1)} %bitcast.75, bf16[16,8,16,64]{3,1,2,0:T(8,128)(2,1)S(1)} %fusion.2), kind=kOutput, calls=%fused_computation.6 | convolution fusion | flops 268435456 | bytes 17563648 | tf_op jit(solution)/shard_map/jtcs,tjsq->tcq/dot_general | solution.py:32
  41.6 0.7 fusion.11
  42.3 0.1 reshape.90
  42.4 0.2 copy.26
  42.6 12.6 %all_to_all.31 = f32[8,64,128]{2,1,0:T(8,128)S(1)} all-to-all(f32[8,64,128]{2,1,0:T(8,128)S(1)} %bitcast.80), channel_id=1, replica_groups=mesh['row'=8,'col'=16] {'row'}, dimensions={0} | all-to-all | bytes 524288 | tf_op jit(solution)/shard_map/all_to_all | solution.py:41
  55.3 8.7 %all_to_all.32 = bf16[8,64,128]{2,1,0:T(8,128)(2,1)S(1)} all-to-all(bf16[8,64,128]{2,1,0:T(8,128)(2,1)S(1)} %broadcast_in_dim.12), channel_id=1, replica_groups=mesh['row'=8,'col'=16] {'row'}, dimensions={0} | all-to-all | bytes 262144 | tf_op jit(solution)/shard_map/all_to_all | solution.py:48
  64.1 0.3 convolution_convert_fusion.2
  64.4 10.2 %fusion = f32[8,16,1024]{2,1,0:T(8,128)S(1)} fusion(bf16[1,1,8,1024,1024]{4,3,2,1,0:T(8,128)(2,1)} %param.7, bf16[8,16,1024]{2,0,1:T(8,128)(2,1)S(1)} %convolution_convert_fusion.2), kind=kOutput, calls=%fused_computation.1 | convolution fusion | flops 268435456 | bytes 17563648 | tf_op jit(solution)/shard_map/tcq,tpq->tcp/dot_general | solution.py:24
  74.6 0.7 fusion.9
  75.3 0.3 reshape.95
  75.5 0.6 copy.64
  76.2 0.2 reshape.96
  76.4 13.6 %all_to_all.33 = f32[16,64,128]{2,1,0:T(8,128)S(1)} all-to-all(f32[16,64,128]{2,1,0:T(8,128)S(1)} %reshape.96), channel_id=1, replica_groups=mesh['row'=8,'col'=16] {'col'}, dimensions={0} | all-to-all | bytes 1048576 | tf_op jit(solution)/shard_map/all_to_all | solution.py:41
  90.1 0.7 divide_convert_fusion.2
  90.9 10.6 %all_to_all.34 = bf16[16,64,128]{2,1,0:T(8,128)(2,1)S(1)} all-to-all(bf16[16,64,128]{2,1,0:T(8,128)(2,1)S(1)} %broadcast_in_dim.14), channel_id=1, replica_groups=mesh['row'=8,'col'=16] {'col'}, dimensions={0} | all-to-all | bytes 524288 | tf_op jit(solution)/shard_map/all_to_all | solution.py:48
  101.5 0.2 reshape.98
  101.7 0.4 fusion.3
  102.1 7.0 %convolution_bitcast_fusion = f32[8,16,1024]{2,1,0:T(8,128)S(1)} fusion(bf16[8,16,64,1024]{3,2,1,0:T(8,128)(2,1)} %bitcast.76, bf16[16,8,16,64]{3,1,2,0:T(8,128)(2,1)S(1)} %fusion.3), kind=kOutput, calls=%fused_computation.5 | convolution fusion | flops 268435456 | bytes 17563648 | tf_op jit(solution)/shard_map/jtcs,tjsq->tcq/dot_general | solution.py:32
  109.1 0.7 fusion.5
  109.8 0.1 reshape.99
  109.9 0.2 copy.35
  110.1 12.2 %all_to_all.35 = f32[8,64,128]{2,1,0:T(8,128)S(1)} all-to-all(f32[8,64,128]{2,1,0:T(8,128)S(1)} %bitcast.81), channel_id=1, replica_groups=mesh['row'=8,'col'=16] {'row'}, dimensions={0} | all-to-all | bytes 524288 | tf_op jit(solution)/shard_map/all_to_all | solution.py:41
  122.3 0.6 divide_log_fusion
  (22 shorter events, 0.7 us)
Async XLA Ops:
  0.6 7.8 %copy-start.2 = (s32[1,1,8,2]{2,3,1,0:T(2,128)S(1)}, s32[1,1,8,2]{2,3,1,0:T(2,128)}, u32[]{:S(2)}) copy-start(s32[1,1,8,2]{2,3,1,0:T(2,128)} %param.6) | copy-start | bytes 196
  8.4 46.8 %copy-start.1 = (f32[4,16,128]{2,1,0:T(8,128)S(1)}, f32[4,16,128]{2,1,0:T(8,128)}, u32[]{:S(2)}) copy-start(f32[4,16,128]{2,1,0:T(8,128)} %param.5) | copy-start | bytes 98308
  41.6 48.5 %copy-start = (f32[8,16,64]{2,1,0:T(8,128)S(1)}, f32[8,16,64]{2,1,0:T(8,128)}, u32[]{:S(2)}) copy-start(f32[8,16,64]{2,1,0:T(8,128)} %param.4) | copy-start | bytes 98308

commit v8 on v7

--- a/solution.py
+++ b/solution.py
@@ -9,7 +9,7 @@
 
 def collect(selector, count, values):
     onehot = (selector[None, :] == jnp.arange(count, dtype=jnp.int32)[:, None]).astype(jnp.float32)
-    return jnp.einsum("rt,tcp->rcp", onehot, values, precision=lax.Precision.HIGHEST)
+    return jnp.einsum("rt,tcp->rcp", onehot, values, precision=lax.Precision.HIGH)
 
 
 def pick(values, selector, axis):

time: 123 us -> 123 us (level)
  no operation moved by 1% of the time
where the time goes in v8:
time: 123 us
  blocking collectives  81.9 us (67%)
  matrix products  26.9 us (22%)
  other arithmetic  8.44 us (7%)
  local copies, waits for them, and re-layouts  4.4 us (4%)
    all_to_all x3, blocking collectives, reduce_scatter(): moved = lax.all_to_all(dense, axis, 0, 0, tiled=True)  38.5 us
    all_to_all x1, blocking collectives, body(): moved = lax.all_to_all(copies, 'col', 0, 0, tiled=True).reshape(n_col, -1)  24.2 us
    all_to_all x2, blocking collectives, all_gather_parts(): moved = lax.all_to_all(copies, axis, 0, 0, tiled=True)  19.2 us
    dot_general x2, matrix products, backward_terms(): jnp.einsum('jtcs,tjsq->tcq', picked, split_tiles, preferred_element_type=...  14.1 us
    dot_general x1, matrix products, forward_terms(): jnp.einsum('tcq,tpq->tcp', picked, tiles, preferred_element_type=jnp.floa...  10.2 us
    reduce_sum x1, other arithmetic, body(): tiles.sum(axis=2, dtype=jnp.float32)[:, None, :]  6.82 us

profile of v8, /device:TPU:1, one launch (start us, length us, event | category | flops | bytes accessed | tf_op | source)
XLA Modules:
  0.0 122.5 jit_solution(10467288916845697575)
XLA Ops:
  0.6 0.9 concatenate.8
  1.6 6.8 %convert_reduce_fusion = f32[8,1024]{1,0:T(8,128)S(1)} fusion(bf16[1,1,8,1024,1024]{4,3,2,1,0:T(8,128)(2,1)} %param.7), kind=kLoop, calls=%fused_computation | loop fusion | flops 16769024 | bytes 16809984 | tf_op jit(solution)/shard_map/reduce_sum | solution.py:67
  8.4 0.1 fusion.19
  8.7 24.2 %all_to_all.30 = f32[16,128,128]{2,1,0:T(8,128)S(1)} all-to-all(f32[16,128,128]{2,1,0:T(8,128)S(1)} %broadcast_in_dim.10), channel_id=1, replica_groups=mesh['row'=8,'col'=16] {'col'}, dimensions={0} | all-to-all | bytes 2097152 | tf_op jit(solution)/shard_map/all_to_all | solution.py:70
  32.8 0.6 copy.63
  33.5 0.1 slice_reduce_fusion
  33.7 0.4 reshape.88
  34.1 0.1 fusion.15
  34.2 0.4 fusion.2
  34.6 7.0 %convolution_bitcast_fusion.1 = f32[8,16,1024]{2,1,0:T(8,128)S(1)} fusion(bf16[8,16,64,1024]{3,2,1,0:T(8,128)(2,1)} %bitcast.75, bf16[16,8,16,64]{3,1,2,0:T(8,128)(2,1)S(1)} %fusion.2), kind=kOutput, calls=%fused_computation.6 | convolution fusion | flops 268435456 | bytes 17563648 | tf_op jit(solution)/shard_map/jtcs,tjsq->tcq/dot_general | solution.py:32
  41.6 0.5 fusion.11
  42.1 0.1 reshape.90
  42.3 0.2 copy.26
  42.4 12.6 %all_to_all.31 = f32[8,64,128]{2,1,0:T(8,128)S(1)} all-to-all(f32[8,64,128]{2,1,0:T(8,128)S(1)} %bitcast.80), channel_id=1, replica_groups=mesh['row'=8,'col'=16] {'row'}, dimensions={0} | all-to-all | bytes 524288 | tf_op jit(solution)/shard_map/all_to_all | solution.py:41
  55.1 8.7 %all_to_all.32 = bf16[8,64,128]{2,1,0:T(8,128)(2,1)S(1)} all-to-all(bf16[8,64,128]{2,1,0:T(8,128)(2,1)S(1)} %broadcast_in_dim.12), channel_id=1, replica_groups=mesh['row'=8,'col'=16] {'row'}, dimensions={0} | all-to-all | bytes 262144 | tf_op jit(solution)/shard_map/all_to_all | solution.py:48
  63.9 0.3 convolution_convert_fusion.2
  64.2 10.2 %fusion = f32[8,16,1024]{2,1,0:T(8,128)S(1)} fusion(bf16[1,1,8,1024,1024]{4,3,2,1,0:T(8,128)(2,1)} %param.7, bf16[8,16,1024]{2,0,1:T(8,128)(2,1)S(1)} %convolution_convert_fusion.2), kind=kOutput, calls=%fused_computation.1 | convolution fusion | flops 268435456 | bytes 17563648 | tf_op jit(solution)/shard_map/tcq,tpq->tcp/dot_general | solution.py:24
  74.4 0.5 fusion.9
  74.9 0.3 reshape.95
  75.2 0.6 copy.64
  75.8 0.2 reshape.96
  76.1 13.6 %all_to_all.33 = f32[16,64,128]{2,1,0:T(8,128)S(1)} all-to-all(f32[16,64,128]{2,1,0:T(8,128)S(1)} %reshape.96), channel_id=1, replica_groups=mesh['row'=8,'col'=16] {'col'}, dimensions={0} | all-to-all | bytes 1048576 | tf_op jit(solution)/shard_map/all_to_all | solution.py:41
  89.8 0.7 divide_convert_fusion.2
  90.6 10.6 %all_to_all.34 = bf16[16,64,128]{2,1,0:T(8,128)(2,1)S(1)} all-to-all(bf16[16,64,128]{2,1,0:T(8,128)(2,1)S(1)} %broadcast_in_dim.14), channel_id=1, replica_groups=mesh['row'=8,'col'=16] {'col'}, dimensions={0} | all-to-all | bytes 524288 | tf_op jit(solution)/shard_map/all_to_all | solution.py:48
  101.2 0.2 reshape.98
  101.4 0.4 fusion.3
  101.8 7.0 %convolution_bitcast_fusion = f32[8,16,1024]{2,1,0:T(8,128)S(1)} fusion(bf16[8,16,64,1024]{3,2,1,0:T(8,128)(2,1)} %bitcast.76, bf16[16,8,16,64]{3,1,2,0:T(8,128)(2,1)S(1)} %fusion.3), kind=kOutput, calls=%fused_computation.5 | convolution fusion | flops 268435456 | bytes 17563648 | tf_op jit(solution)/shard_map/jtcs,tjsq->tcq/dot_general | solution.py:32
  108.8 0.5 fusion.5
  109.3 0.1 reshape.99
  109.5 0.2 copy.35
  109.6 12.2 %all_to_all.35 = f32[8,64,128]{2,1,0:T(8,128)S(1)} all-to-all(f32[8,64,128]{2,1,0:T(8,128)S(1)} %bitcast.81), channel_id=1, replica_groups=mesh['row'=8,'col'=16] {'row'}, dimensions={0} | all-to-all | bytes 524288 | tf_op jit(solution)/shard_map/all_to_all | solution.py:41
  121.9 0.6 divide_log_fusion
  (22 shorter events, 0.7 us)
Async XLA Ops:
  0.6 7.8 %copy-start.2 = (s32[1,1,8,2]{2,3,1,0:T(2,128)S(1)}, s32[1,1,8,2]{2,3,1,0:T(2,128)}, u32[]{:S(2)}) copy-start(s32[1,1,8,2]{2,3,1,0:T(2,128)} %param.6) | copy-start | bytes 196
  8.4 46.7 %copy-start.1 = (f32[4,16,128]{2,1,0:T(8,128)S(1)}, f32[4,16,128]{2,1,0:T(8,128)}, u32[]{:S(2)}) copy-start(f32[4,16,128]{2,1,0:T(8,128)} %param.5) | copy-start | bytes 98308
  41.6 48.2 %copy-start = (f32[8,16,64]{2,1,0:T(8,128)S(1)}, f32[8,16,64]{2,1,0:T(8,128)}, u32[]{:S(2)}) copy-start(f32[8,16,64]{2,1,0:T(8,128)} %param.4) | copy-start | bytes 98308
